TPU v7x, 32 devices: a whole 2x2x4 slice. The times are simulated.
32 devices in a mesh: gx: 8 (over y, x, core), gy: 4 (over z).
Axes of the slice: x: 2, y: 2, z: 4, core: 2. Of those that a mesh axis runs over, the one named last changes fastest.
Arguments:
- positions: float32 [3, 65536], P(None, ('gx', 'gy')), may hold values from 0 to 8, as said below
- density: float32 [65536], P(('gx', 'gy')), may hold values from 0.5 to 4
- momentum: float32 [3, 65536], P(None, ('gx', 'gy')), may hold values from -3 to 3
- field: float32 [3, 65536], P(None, ('gx', 'gy')), may hold values from -3 to 3
- psi: float32 [65536], P(('gx', 'gy')), may hold values from -3 to 3
- ohmic: float32 [65536], P(('gx', 'gy')), may hold values from 0.05 to 20
- ambipolar: float32 [65536], P(('gx', 'gy')), may hold values from 0.02 to 0.3
- ghost_index: int32 [34816], P(('gx', 'gy')), may hold values from 0 to 2047, as said below
- tile_i: int32 [2048], P(('gx', 'gy')), may hold values from 0 to 15, as said below
- tile_j: int32 [2048], P(('gx', 'gy')), may hold values from 0 to 24, as said below
- tile_count: int32 [32], P(('gx', 'gy')), may hold values from 16 to 64, as said below
Outputs:
- density_new: float32 [65536], P(('gx', 'gy'))
- momentum_new: float32 [3, 65536], P(None, ('gx', 'gy'))
- field_new: float32 [3, 65536], P(None, ('gx', 'gy'))
- psi_new: float32 [65536], P(('gx', 'gy'))
Inputs may be any that keep to these rules, and one draw needn't show every extreme that they name: `positions`: x lies in [ix, ix+1) and y in [iy, iy+1) for the owner (ix, iy); z lies in [0, 0.5). `ghost_index`: within one device the 1088 numbers are distinct. `tile_i`: a block of 128 local particles. `tile_j`: a block of 128 in the extended set; the pairs (tile_i, tile_j) of one device are distinct. `tile_count`: the devices of a dense region of three by three slabs use all 64 entries.
All inputs are finite; a program needn't handle non-finite values.
Results may differ from a plain program's by a relative error of at most 0.0003.
Values sent between devices are 32-bit elements; how exact they have to be, the bound alone decides.
No kernel may reach another device: no remote copies, remote signals or barrier semaphores. Data moves between devices by JAX's collectives and lax.ppermute only.
A program may use at most 64 MiB of HBM per device.

v0:
```python
import math

import jax
import jax.numpy as jnp
from jax import lax
from jax.sharding import PartitionSpec as P

TILE = 128
SECTIONS = 4
GHOST_X = 320
GHOST_Y = 160
GHOST_C = 32
EXT_BLOCKS = 25


DIRECTIONS = [(-1, -1), (-1, 0), (-1, 1), (0, -1), (0, 1), (1, -1), (1, 0), (1, 1)]
courant = 0.3
damping = 0.5


def extended(array, sides, width):
    for axis, dim in sides:
        size, length = (lax.axis_size(axis), array.shape[dim])
        up = [(i, (i + 1) % size) for i in range(size - 1)]
        down = [(j, i) for i, j in up]
        last = lax.slice_in_dim(array, length - width, length, axis=dim)
        leading = lax.slice_in_dim(array, 0, width, axis=dim)
        before = lax.ppermute(last, axis, up)
        after = lax.ppermute(leading, axis, down)
        array = jnp.concatenate([before, array, after], axis=dim)
    return array


def mesh_max(value):
    for axis in ("gy", "gx"):
        size = lax.axis_size(axis)
        shift = 1
        while shift < size:
            pairs = [(i, (i + shift) % size) for i in range(size)]
            value = jnp.maximum(value, lax.ppermute(value, axis, pairs))
            shift = shift * 2
    return value


def ghost_sizes():
    return [GHOST_C, GHOST_X, GHOST_C, GHOST_Y, GHOST_Y, GHOST_C, GHOST_X, GHOST_C]


def ghost_offsets():
    sizes = ghost_sizes()
    starts = [0]
    for value in sizes[:-1]:
        starts.append(starts[-1] + value)
    return starts


def rkl_table(sections):
    wfirst = 4.0 / (sections * sections + sections - 2)
    bvals = [1.0 / 3.0, 1.0 / 3.0, 1.0 / 3.0] + [
        (j * j + j - 2) / (2.0 * j * (j + 1)) for j in range(3, sections + 1)
    ]
    first = bvals[1] * wfirst
    rows = []
    for j in range(2, sections + 1):
        mu_j = (2.0 * j - 1.0) / j * bvals[j] / bvals[j - 1]
        nu_j = -(j - 1.0) / j * bvals[j] / bvals[j - 2]
        mut_j = mu_j * wfirst
        rows.append((mu_j, nu_j, mut_j, -(1.0 - bvals[j - 1]) * mut_j))
    return (first, rows)


def kernel_tile(near, far):
    dist = (near[0][..., :, None] - far[0][..., None, :]) ** 2
    dist = dist + (near[1][..., :, None] - far[1][..., None, :]) ** 2
    dist = dist + (near[2][..., :, None] - far[2][..., None, :]) ** 2
    base = jnp.maximum(1.0 - 4.0 * dist, 0.0)
    return base * base


def flux_rows(ext):
    posit = ext[0:3]
    live = ext[3]
    rho = ext[4]
    vel = ext[5:8]
    bfl = ext[8:11]
    cpsi = ext[11]
    speed = ext[12]
    mom = rho * vel
    ptot = rho + 0.5 * jnp.sum(bfl * bfl, axis=0)
    fluxes = []
    for d in range(3):
        rows_d = [mom[d]]
        for k in range(3):
            term = mom[k] * vel[d] - bfl[k] * bfl[d]
            rows_d.append(term + ptot if k == d else term)
        for k in range(3):
            term = vel[d] * bfl[k] - bfl[d] * vel[k]
            rows_d.append(term + cpsi if k == d else term)
        rows_d.append(bfl[d])
        fluxes.append(jnp.stack(rows_d))
    flux = jnp.stack(fluxes)
    state = jnp.concatenate([rho[None], mom, bfl, cpsi[None]], axis=0)
    gsum = posit[0] * flux[0] + posit[1] * flux[1] + posit[2] * flux[2]
    return jnp.concatenate(
        [live[None], posit, flux.reshape(24, -1), gsum, speed * state, speed[None], state], axis=0
    )


def hydro_rate(acc, local, ch):
    count_n = acc[0]
    num = acc.shape[1]
    wflux = acc[4:28].reshape(3, 8, num)
    flux = local[4:28].reshape(3, 8, num)
    posit = local[1:4]
    speed = local[44]
    state = local[45:53]
    central = acc[28:36]
    for d in range(3):
        central = central + flux[d] * (acc[1 + d] - posit[d] * count_n) - posit[d] * wflux[d]
    central = jnp.concatenate([central[:7], (ch * ch) * central[7:8]], axis=0)
    dissip = speed * (acc[45:53] - state * count_n) + acc[36:44] - state * acc[44]
    return ((0.5 * dissip - 0.5 * central) / (1.0 + count_n), count_n)


def diffusion_rate(acc, bloc, etaloc, count_n):
    return 0.5 * (etaloc * (acc[0:3] - bloc * count_n) + acc[3:6] - bloc * acc[6]) / (1.0 + count_n)


def spread_ghosts(rows, ghost_index):
    sizes = ghost_sizes()
    starts = ghost_offsets()
    sends = [
        jnp.take(rows, ghost_index[starts[d] : starts[d] + sizes[d]], axis=1) for d in range(8)
    ]

    def toward(p, q):
        return sends[DIRECTIONS.index((p, q))]

    got = {}
    face_x = GHOST_X
    corner = GHOST_C
    face_y = GHOST_Y
    toward_low = jnp.concatenate([toward(-1, 0), toward(-1, -1), toward(-1, 1)], axis=1)
    toward_high = jnp.concatenate([toward(1, 0), toward(1, -1), toward(1, 1)], axis=1)
    along_x = extended(jnp.stack([toward_low, toward_high]), (("gx", 0),), 1)
    from_low = along_x[0]
    from_high = along_x[3]
    downward = jnp.concatenate(
        [
            toward(0, -1),
            from_low[:, face_x : face_x + corner],
            from_high[:, face_x : face_x + corner],
        ],
        axis=1,
    )
    upward = jnp.concatenate(
        [toward(0, 1), from_low[:, face_x + corner :], from_high[:, face_x + corner :]], axis=1
    )
    along_y = extended(jnp.stack([downward, upward]), (("gy", 0),), 1)
    from_below = along_y[0]
    from_above = along_y[3]
    got[-1, 0] = from_low[:, :face_x]
    got[1, 0] = from_high[:, :face_x]
    got[0, -1] = from_below[:, :face_y]
    got[0, 1] = from_above[:, :face_y]
    got[-1, -1] = from_below[:, face_y : face_y + corner]
    got[1, -1] = from_below[:, face_y + corner :]
    got[-1, 1] = from_above[:, face_y : face_y + corner]
    got[1, 1] = from_above[:, face_y + corner :]
    return jnp.concatenate([got[p, q] for p, q in DIRECTIONS], axis=1)


def extend(rows, extra):
    filler = jnp.zeros(
        (rows.shape[0], EXT_BLOCKS * TILE - rows.shape[1] - extra.shape[1]), jnp.float32
    )
    return jnp.concatenate([rows, extra, filler], axis=1)


def shards(
    positions,
    density,
    momentum,
    field,
    psi,
    ohmic,
    ambipolar,
    ghost_index,
    tile_i,
    tile_j,
    tile_count,
):
    nlocal = density.shape[0]
    nblocks = nlocal // TILE
    velocity = momentum / density
    speed = jnp.sqrt(1.0 + jnp.sum(field * field, axis=0) / density)
    fac = ambipolar / (density * jnp.sqrt(density))
    live = jnp.ones_like(density)
    core_rows = [positions, live[None], density[None], velocity, field, psi[None], speed[None]]
    payload = jnp.concatenate(core_rows + [ohmic[None], fac[None]], axis=0)
    ch = mesh_max(jnp.max(speed))
    dt = courant / ch
    ghosts = spread_ghosts(payload, ghost_index)
    ext = extend(payload, ghosts)
    pos_blocks = ext[0:3].reshape(3, EXT_BLOCKS, TILE)
    qext = flux_rows(ext)
    q_blocks = qext.reshape(qext.shape[0], EXT_BLOCKS, TILE)
    count = tile_count[0]
    tiles_total = tile_i.shape[0]
    batch = math.gcd(32, tiles_total)
    rounds = (count + batch - 1) // batch
    block_ids = jnp.arange(nblocks, dtype=jnp.int32)

    def batch_lists(offset):
        near_ids = lax.dynamic_slice_in_dim(tile_i, offset, batch, 0)
        far_ids = lax.dynamic_slice_in_dim(tile_j, offset, batch, 0)
        usable = offset + jnp.arange(batch, dtype=jnp.int32) < count
        onehot = ((near_ids[None, :] == block_ids[:, None]) & usable[None, :]).astype(jnp.float32)
        return (near_ids, far_ids, onehot)

    def fold_batch(acc, blocks, weight, far_ids, onehot):
        qsel = jnp.take(blocks, far_ids, axis=1)
        part = jnp.einsum(
            "rtb,tab->rta",
            qsel,
            weight,
            precision=lax.Precision.HIGH,
            preferred_element_type=jnp.float32,
        )
        return acc + jnp.einsum(
            "pt,rta->rpa",
            onehot,
            part,
            precision=lax.Precision.HIGHEST,
            preferred_element_type=jnp.float32,
        )

    def hydro_step(turn, carry):
        acc, stored = carry
        offset = (turn * batch).astype(jnp.int32)
        near_ids, far_ids, onehot = batch_lists(offset)
        near = jnp.take(pos_blocks, near_ids, axis=1)
        far = jnp.take(pos_blocks, far_ids, axis=1)
        weight = kernel_tile(near, far)
        stored = lax.dynamic_update_slice_in_dim(stored, weight, offset, 0)
        return (fold_batch(acc, q_blocks, weight, far_ids, onehot), stored)

    acc_start = jnp.zeros((qext.shape[0], nblocks, TILE), jnp.float32)
    stored_start = jnp.zeros((tiles_total, TILE, TILE), jnp.float32)
    acc, stored = lax.fori_loop(0, rounds, hydro_step, (acc_start, stored_start))
    acc = acc.reshape(qext.shape[0], nlocal)
    rate, count_n = hydro_rate(acc, qext[:, :nlocal], ch)
    density_new = density + dt * rate[0]
    momentum_new = momentum + dt * rate[1:4]
    yzero = field + dt * rate[4:7]
    psi_new = (psi + dt * rate[7]) * jnp.exp(-damping * dt * ch)

    def operator(bfl):
        eta = ohmic + fac * jnp.sum(bfl * bfl, axis=0)
        ghost_b = spread_ghosts(bfl, ghost_index)
        ghost_eta = ghosts[13] + ghosts[14] * jnp.sum(ghost_b * ghost_b, axis=0)
        b_ext = extend(bfl, ghost_b)
        eta_ext = extend(eta[None], ghost_eta[None])[0]
        qdiff = jnp.concatenate([b_ext, eta_ext[None] * b_ext, eta_ext[None]], axis=0)
        diff_blocks = qdiff.reshape(7, EXT_BLOCKS, TILE)

        def diff_step(turn, acc_diff):
            offset = (turn * batch).astype(jnp.int32)
            near_ids, far_ids, onehot = batch_lists(offset)
            weight = lax.dynamic_slice_in_dim(stored, offset, batch, 0)
            return fold_batch(acc_diff, diff_blocks, weight, far_ids, onehot)

        acc_diff = lax.fori_loop(0, rounds, diff_step, jnp.zeros((7, nblocks, TILE), jnp.float32))
        return diffusion_rate(acc_diff.reshape(7, nlocal), bfl, eta, count_n)

    first, rows = rkl_table(SECTIONS)
    lzero = operator(yzero)
    older = yzero
    prev = yzero + first * dt * lzero
    for mu_j, nu_j, mut_j, gam_j in rows:
        nxt = (
            mu_j * prev
            + nu_j * older
            + (1.0 - mu_j - nu_j) * yzero
            + mut_j * dt * operator(prev)
            + gam_j * dt * lzero
        )
        older = prev
        prev = nxt
    return (density_new, momentum_new, prev, psi_new)


def solution(mesh):
    placed = (
        P(None, ("gx", "gy")),
        P(("gx", "gy")),
        P(None, ("gx", "gy")),
        P(None, ("gx", "gy")),
        P(("gx", "gy")),
        P(("gx", "gy")),
        P(("gx", "gy")),
        P(("gx", "gy")),
        P(("gx", "gy")),
        P(("gx", "gy")),
        P(("gx", "gy")),
    )
    return jax.shard_map(
        shards,
        mesh=mesh,
        in_specs=placed,
        out_specs=(P(("gx", "gy")), P(None, ("gx", "gy")), P(None, ("gx", "gy")), P(("gx", "gy"))),
        check_vma=False,
    )
```

profile of v0, /device:TPU:30, one launch (start us, length us, event | category | flops | bytes accessed | tf_op | source)
XLA Modules:
  0.0 215.0 jit_solution(2500106323844763308)
XLA Ops:
  15.9 3.6 %collective-permute-start.6 = (f32[1,15,384]{2,1,0:T(8,128)S(1)}, f32[1,15,384]{2,1,0:T(8,128)S(1)}, u32[]{:S(2)}, u32[]{:S(2)}) collective-permute-start(f32[1,15,384]{2,1,0:T(8,128)S(1)} %maximum_bitcast_fusion.1), channel_id=1, source_target_pairs={{4,0},{8,4},{12,8},{16,12},{20,16},{24,20},{28,24},{5,1},{9,5},{13... | collective-permute-start | bytes 69128 | tf_op jit(solution)/shard_map/ppermute | solution.py:29
  34.8 2.5 %collective-permute-done.3 = f32[]{:T(128)} collective-permute-done((f32[]{:T(128)}, f32[]{:T(128)}, u32[]{:S(2)}, u32[]{:S(2)}) %collective-permute-start.3) | collective-permute-done | bytes 36 | tf_op jit(solution)/shard_map/ppermute | solution.py:40
  38.0 2.6 %collective-permute-start.4 = (f32[]{:T(128)}, f32[]{:T(128)}, u32[]{:S(2)}, u32[]{:S(2)}) collective-permute-start(f32[]{:T(128)} %max.21), channel_id=1, source_target_pairs={{0,16},{4,20},{8,24},{12,28},{16,0},{20,4},{24,8},{28,12},{1,17},{... | collective-permute-start | bytes 20 | tf_op jit(solution)/shard_map/ppermute | solution.py:40
  42.6 2.8 %collective-permute-start.8 = (f32[1,15,224]{2,1,0:T(8,128)S(1)}, f32[1,15,224]{2,1,0:T(8,128)S(1)}, u32[]{:S(2)}, u32[]{:S(2)}) collective-permute-start(f32[1,15,224]{2,1,0:T(8,128)S(1)} %maximum_bitcast_fusion.3), channel_id=1, source_target_pairs={{1,0},{2,1},{3,2},{5,4},{6,5},{7,6},{9,8},{10,9},{11,10},{13,12},{... | collective-permute-start | bytes 40328 | tf_op jit(solution)/shard_map/ppermute | solution.py:29
  46.9 4.2 %collective-permute-done.7 = f32[1,15,224]{2,1,0:T(8,128)S(1)} collective-permute-done((f32[1,15,224]{2,1,0:T(8,128)S(1)}, f32[1,15,224]{2,1,0:T(8,128)S(1)}, u32[]{:S(2)}, u32[]{:S(2)}) %collective-permute-start.7) | collective-permute-done | bytes 13472 | tf_op jit(solution)/shard_map/ppermute | solution.py:28
  54.4 2.4 %broadcast_in_dim.153 = f32[64,128,128]{2,1,0:T(8,128)} broadcast(f32[]{:T(128)} %constant.71.clone.1), dimensions={} | broadcast | bytes 4194308 | tf_op jit(solution)/shard_map/broadcast_in_dim | solution.py:249
  56.9 23.1 %while.57 = (s32[]{:T(128)}, f32[53,16,128]{2,1,0:T(8,128)S(1)}, f32[64,128,128]{2,1,0:T(8,128)}, s32[]{:T(128)}, s32[64]{0:T(128)S(1)}, /*index=5*/f32[3,25,128...) while((s32[]{:T(128)}, f32[53,16,128]{2,1,0:T(8,128)S(1)}, ...), condition=%wide.region_4.9_spmd.clone, body=%wide.region_3.8_spmd.clone.sunk | while | flops 221341216 | bytes 8103835 | solution.py:250
  58.6 3.1 %fusion.223 = f32[64,128,128]{2,1,0:T(8,128)} fusion(f32[64,128,128]{2,1,0:T(8,128)} %get-tuple-element.1048, s32[]{:T(128)S(6)} %select_n.425, f32[32,128]{1,0:T(8,128)S(1)} %bitcast.552, f32[32,128]{1,0:T(8,128)S(1)} %bitcast.558, f32[32,128]{1,0:T(8,128)S(1)} %bitcast.554, f32[32,128]{1,0:T(8,128)S(1)} %bitcast.560, f32[32,128]{1,0:T(8,128)S(1)} %bitcast.550, ...), kind=kLoop, calls=%fused_computation.53.clone.1 | loop fusion | flops 6291456 | bytes 2195460 | tf_op jit(solution)/shard_map/while/body/dynamic_update_slice | solution.py:245
  62.3 4.9 %fusion.221 = f32[53,32,128]{2,0,1:T(8,128)S(1)} fusion(f32[32,128]{1,0:T(8,128)S(1)} %bitcast.553, f32[32,128]{1,0:T(8,128)S(1)} %bitcast.559, f32[32,128]{1,0:T(8,128)S(1)} %bitcast.555, f32[32,128]{1,0:T(8,128)S(1)} %bitcast.561, f32[32,128]{1,0:T(8,128)S(1)} %bitcast.551, f32[32,128]{1,0:T(8,128)S(1)} %bitcast.557, ...), kind=kOutput, calls=%fused_computation.55.clone.1 | convolution fusion | flops 173232128 | bytes 1835040 | tf_op jit(solution)/shard_map/while/body/rtb,tab->rta/dot_general | solution.py:223
  70.1 3.1 %fusion.223 = f32[64,128,128]{2,1,0:T(8,128)} fusion(f32[64,128,128]{2,1,0:T(8,128)} %get-tuple-element.1048, s32[]{:T(128)S(6)} %select_n.425, f32[32,128]{1,0:T(8,128)S(1)} %bitcast.552, f32[32,128]{1,0:T(8,128)S(1)} %bitcast.558, f32[32,128]{1,0:T(8,128)S(1)} %bitcast.554, f32[32,128]{1,0:T(8,128)S(1)} %bitcast.560, f32[32,128]{1,0:T(8,128)S(1)} %bitcast.550, ...), kind=kLoop, calls=%fused_computation.53.clone.1 | loop fusion | flops 6291456 | bytes 2195460 | tf_op jit(solution)/shard_map/while/body/dynamic_update_slice | solution.py:245
  73.8 4.9 %fusion.221 = f32[53,32,128]{2,0,1:T(8,128)S(1)} fusion(f32[32,128]{1,0:T(8,128)S(1)} %bitcast.553, f32[32,128]{1,0:T(8,128)S(1)} %bitcast.559, f32[32,128]{1,0:T(8,128)S(1)} %bitcast.555, f32[32,128]{1,0:T(8,128)S(1)} %bitcast.561, f32[32,128]{1,0:T(8,128)S(1)} %bitcast.551, f32[32,128]{1,0:T(8,128)S(1)} %bitcast.557, ...), kind=kOutput, calls=%fused_computation.55.clone.1 | convolution fusion | flops 173232128 | bytes 1835040 | tf_op jit(solution)/shard_map/while/body/rtb,tab->rta/dot_general | solution.py:223
  90.6 3.6 %collective-permute-start.10 = (f32[1,3,384]{2,1,0:T(4,128)S(1)}, f32[1,3,384]{2,1,0:T(4,128)S(1)}, u32[]{:S(2)}, u32[]{:S(2)}) collective-permute-start(f32[1,3,384]{2,1,0:T(4,128)S(1)} %maximum_bitcast_fusion.5), channel_id=1, source_target_pairs={{4,0},{8,4},{12,8},{16,12},{20,16},{24,20},{28,24},{5,1},{9,5},{13... | collective-permute-start | bytes 13832 | tf_op jit(solution)/shard_map/ppermute | solution.py:29
  99.9 4.1 %collective-permute-done.11 = f32[1,3,224]{2,1,0:T(4,128)S(1)} collective-permute-done((f32[1,3,224]{2,1,0:T(4,128)S(1)}, f32[1,3,224]{2,1,0:T(4,128)S(1)}, u32[]{:S(2)}, u32[]{:S(2)}) %collective-permute-start.11) | collective-permute-done | bytes 2720 | tf_op jit(solution)/shard_map/ppermute | solution.py:28
  104.6 10.2 %while.58 = (s32[]{:T(128)}, f32[7,16,128]{2,1,0:T(8,128)S(1)}, s32[]{:T(128)}, f32[64,128,128]{2,1,0:T(8,128)}, s32[64]{0:T(128)S(1)}, /*index=5*/f32[7,25,128]...) while((s32[]{:T(128)}, f32[7,16,128]{2,1,0:T(8,128)S(1)}, ...), condition=%wide.region_8.17_spmd.clone, body=%wide.region_7.0_spmd.clone.sunk | while | flops 27570436 | bytes 2790583 | solution.py:273
  106.1 3.4 %fusion.228 = f32[7,32,128]{2,0,1:T(8,128)S(1)} fusion(f32[64,128,128]{2,1,0:T(8,128)} %get-tuple-element.1099, s32[]{:T(128)S(6)} %select_n.427, f32[32,7,128]{2,1,0:T(8,128)S(1)} %gather_fusion.3, pred[32]{0:T(512)(128)(4,1)S(1)} %get-tuple-element.998), kind=kOutput, calls=%fused_computation.92.clone.1 | convolution fusion | flops 22048768 | bytes 2326564 | tf_op jit(solution)/shard_map/while/body/rtb,tab->rta/dot_general | solution.py:223
  111.1 3.4 %fusion.228 = f32[7,32,128]{2,0,1:T(8,128)S(1)} fusion(f32[64,128,128]{2,1,0:T(8,128)} %get-tuple-element.1099, s32[]{:T(128)S(6)} %select_n.427, f32[32,7,128]{2,1,0:T(8,128)S(1)} %gather_fusion.3, pred[32]{0:T(512)(128)(4,1)S(1)} %get-tuple-element.998), kind=kOutput, calls=%fused_computation.92.clone.1 | convolution fusion | flops 22048768 | bytes 2326564 | tf_op jit(solution)/shard_map/while/body/rtb,tab->rta/dot_general | solution.py:223
  124.2 3.6 %collective-permute-start.14 = (f32[1,3,384]{2,1,0:T(4,128)S(1)}, f32[1,3,384]{2,1,0:T(4,128)S(1)}, u32[]{:S(2)}, u32[]{:S(2)}) collective-permute-start(f32[1,3,384]{2,1,0:T(4,128)S(1)} %maximum_bitcast_fusion.7), channel_id=1, source_target_pairs={{4,0},{8,4},{12,8},{16,12},{20,16},{24,20},{28,24},{5,1},{9,5},{13... | collective-permute-start | bytes 13832 | tf_op jit(solution)/shard_map/ppermute | solution.py:29
  129.3 3.7 %collective-permute-start.16 = (f32[1,3,224]{2,1,0:T(4,128)S(1)}, f32[1,3,224]{2,1,0:T(4,128)S(1)}, u32[]{:S(2)}, u32[]{:S(2)}) collective-permute-start(f32[1,3,224]{2,1,0:T(4,128)S(1)} %maximum_bitcast_fusion.15), channel_id=1, source_target_pairs={{1,0},{2,1},{3,2},{5,4},{6,5},{7,6},{9,8},{10,9},{11,10},{13,12},{... | collective-permute-start | bytes 8072 | tf_op jit(solution)/shard_map/ppermute | solution.py:29
  134.4 4.1 %collective-permute-done.15 = f32[1,3,224]{2,1,0:T(4,128)S(1)} collective-permute-done((f32[1,3,224]{2,1,0:T(4,128)S(1)}, f32[1,3,224]{2,1,0:T(4,128)S(1)}, u32[]{:S(2)}, u32[]{:S(2)}) %collective-permute-start.15) | collective-permute-done | bytes 2720 | tf_op jit(solution)/shard_map/ppermute | solution.py:28
  139.1 10.0 %while.59 = (s32[]{:T(128)}, f32[7,16,128]{2,1,0:T(8,128)S(1)}, s32[]{:T(128)}, f32[64,128,128]{2,1,0:T(8,128)}, s32[64]{0:T(128)S(1)}, /*index=5*/f32[7,25,128]...) while((s32[]{:T(128)}, f32[7,16,128]{2,1,0:T(8,128)S(1)}, ...), condition=%wide.region_12.21_spmd.clone, body=%wide.region_11.20_spmd.clone.sunk | while | flops 27570436 | bytes 2790583 | solution.py:273
  140.5 3.4 %fusion.234 = f32[7,32,128]{2,0,1:T(8,128)S(1)} fusion(f32[64,128,128]{2,1,0:T(8,128)} %get-tuple-element.1135, s32[]{:T(128)S(6)} %select_n.429, f32[32,7,128]{2,1,0:T(8,128)S(1)} %gather_fusion.4, pred[32]{0:T(512)(128)(4,1)S(1)} %get-tuple-element.1009), kind=kOutput, calls=%fused_computation.113.clone.1 | convolution fusion | flops 22048768 | bytes 2326564 | tf_op jit(solution)/shard_map/while/body/rtb,tab->rta/dot_general | solution.py:223
  145.4 3.4 %fusion.234 = f32[7,32,128]{2,0,1:T(8,128)S(1)} fusion(f32[64,128,128]{2,1,0:T(8,128)} %get-tuple-element.1135, s32[]{:T(128)S(6)} %select_n.429, f32[32,7,128]{2,1,0:T(8,128)S(1)} %gather_fusion.4, pred[32]{0:T(512)(128)(4,1)S(1)} %get-tuple-element.1009), kind=kOutput, calls=%fused_computation.113.clone.1 | convolution fusion | flops 22048768 | bytes 2326564 | tf_op jit(solution)/shard_map/while/body/rtb,tab->rta/dot_general | solution.py:223
  158.5 3.6 %collective-permute-start.18 = (f32[1,3,384]{2,1,0:T(4,128)S(1)}, f32[1,3,384]{2,1,0:T(4,128)S(1)}, u32[]{:S(2)}, u32[]{:S(2)}) collective-permute-start(f32[1,3,384]{2,1,0:T(4,128)S(1)} %maximum_bitcast_fusion.9), channel_id=1, source_target_pairs={{4,0},{8,4},{12,8},{16,12},{20,16},{24,20},{28,24},{5,1},{9,5},{13... | collective-permute-start | bytes 13832 | tf_op jit(solution)/shard_map/ppermute | solution.py:29
  167.0 4.1 %collective-permute-done.19 = f32[1,3,224]{2,1,0:T(4,128)S(1)} collective-permute-done((f32[1,3,224]{2,1,0:T(4,128)S(1)}, f32[1,3,224]{2,1,0:T(4,128)S(1)}, u32[]{:S(2)}, u32[]{:S(2)}) %collective-permute-start.19) | collective-permute-done | bytes 2720 | tf_op jit(solution)/shard_map/ppermute | solution.py:28
  171.7 10.0 %while.60 = (s32[]{:T(128)}, f32[7,16,128]{2,1,0:T(8,128)S(1)}, s32[]{:T(128)}, f32[64,128,128]{2,1,0:T(8,128)}, s32[64]{0:T(128)S(1)}, /*index=5*/f32[7,25,128]...) while((s32[]{:T(128)}, f32[7,16,128]{2,1,0:T(8,128)S(1)}, ...), condition=%wide.region_16.25_spmd.clone, body=%wide.region_15.24_spmd.clone.sunk | while | flops 27570436 | bytes 2790583 | solution.py:273
  173.1 3.4 %fusion.240 = f32[7,32,128]{2,0,1:T(8,128)S(1)} fusion(f32[64,128,128]{2,1,0:T(8,128)} %get-tuple-element.1171, s32[]{:T(128)S(6)} %select_n.431, f32[32,7,128]{2,1,0:T(8,128)S(1)} %gather_fusion.5, pred[32]{0:T(512)(128)(4,1)S(1)} %get-tuple-element.1020), kind=kOutput, calls=%fused_computation.134.clone.1 | convolution fusion | flops 22048768 | bytes 2326564 | tf_op jit(solution)/shard_map/while/body/rtb,tab->rta/dot_general | solution.py:223
  178.1 3.4 %fusion.240 = f32[7,32,128]{2,0,1:T(8,128)S(1)} fusion(f32[64,128,128]{2,1,0:T(8,128)} %get-tuple-element.1171, s32[]{:T(128)S(6)} %select_n.431, f32[32,7,128]{2,1,0:T(8,128)S(1)} %gather_fusion.5, pred[32]{0:T(512)(128)(4,1)S(1)} %get-tuple-element.1020), kind=kOutput, calls=%fused_computation.134.clone.1 | convolution fusion | flops 22048768 | bytes 2326564 | tf_op jit(solution)/shard_map/while/body/rtb,tab->rta/dot_general | solution.py:223
  191.2 3.6 %collective-permute-start.22 = (f32[1,3,384]{2,1,0:T(4,128)S(1)}, f32[1,3,384]{2,1,0:T(4,128)S(1)}, u32[]{:S(2)}, u32[]{:S(2)}) collective-permute-start(f32[1,3,384]{2,1,0:T(4,128)S(1)} %maximum_bitcast_fusion.11), channel_id=1, source_target_pairs={{4,0},{8,4},{12,8},{16,12},{20,16},{24,20},{28,24},{5,1},{9,5},{13... | collective-permute-start | bytes 13832 | tf_op jit(solution)/shard_map/ppermute | solution.py:29
  199.7 4.1 %collective-permute-done.23 = f32[1,3,224]{2,1,0:T(4,128)S(1)} collective-permute-done((f32[1,3,224]{2,1,0:T(4,128)S(1)}, f32[1,3,224]{2,1,0:T(4,128)S(1)}, u32[]{:S(2)}, u32[]{:S(2)}) %collective-permute-start.23) | collective-permute-done | bytes 2720 | tf_op jit(solution)/shard_map/ppermute | solution.py:28
  204.3 10.0 %while.61 = (s32[]{:T(128)}, f32[7,16,128]{2,1,0:T(8,128)S(1)}, s32[]{:T(128)}, f32[64,128,128]{2,1,0:T(8,128)}, s32[64]{0:T(128)S(1)}, /*index=5*/f32[7,25,128]...) while((s32[]{:T(128)}, f32[7,16,128]{2,1,0:T(8,128)S(1)}, ...), condition=%wide.region_20.29_spmd.clone, body=%wide.region_19.28_spmd.clone.sunk | while | flops 27570436 | bytes 2790583 | solution.py:273
  205.7 3.4 %fusion.246 = f32[7,32,128]{2,0,1:T(8,128)S(1)} fusion(f32[64,128,128]{2,1,0:T(8,128)} %get-tuple-element.1207, s32[]{:T(128)S(6)} %select_n.433, f32[32,7,128]{2,1,0:T(8,128)S(1)} %gather_fusion.6, pred[32]{0:T(512)(128)(4,1)S(1)} %get-tuple-element.1031), kind=kOutput, calls=%fused_computation.155.clone.1 | convolution fusion | flops 22048768 | bytes 2326564 | tf_op jit(solution)/shard_map/while/body/rtb,tab->rta/dot_general | solution.py:223
  210.7 3.4 %fusion.246 = f32[7,32,128]{2,0,1:T(8,128)S(1)} fusion(f32[64,128,128]{2,1,0:T(8,128)} %get-tuple-element.1207, s32[]{:T(128)S(6)} %select_n.433, f32[32,7,128]{2,1,0:T(8,128)S(1)} %gather_fusion.6, pred[32]{0:T(512)(128)(4,1)S(1)} %get-tuple-element.1031), kind=kOutput, calls=%fused_computation.155.clone.1 | convolution fusion | flops 22048768 | bytes 2326564 | tf_op jit(solution)/shard_map/while/body/rtb,tab->rta/dot_general | solution.py:223
  (420 shorter events, 111.4 us)
Async XLA Ops:
  0.6 19.2 %copy-start.7 = (s32[1088]{0:T(1024)S(1)}, s32[1088]{0:T(1024)}, u32[]{:S(2)}) copy-start(s32[1088]{0:T(1024)} %param.44) | copy-start | bytes 13060
  11.0 31.3 %collective-permute-start.5 = (f32[1,15,384]{2,1,0:T(8,128)S(1)}, f32[1,15,384]{2,1,0:T(8,128)S(1)}, u32[]{:S(2)}, u32[]{:S(2)}) collective-permute-start(f32[1,15,384]{2,1,0:T(8,128)S(1)} %maximum_bitcast_fusion), channel_id=1, source_target_pairs={{0,4},{4,8},{8,12},{12,16},{16,20},{20,24},{24,28},{1,5},{5,9},{9,... | collective-permute-start | bytes 69128 | tf_op jit(solution)/shard_map/ppermute | solution.py:28
  15.9 26.6 %collective-permute-start.6 = (f32[1,15,384]{2,1,0:T(8,128)S(1)}, f32[1,15,384]{2,1,0:T(8,128)S(1)}, u32[]{:S(2)}, u32[]{:S(2)}) collective-permute-start(f32[1,15,384]{2,1,0:T(8,128)S(1)} %maximum_bitcast_fusion.1), channel_id=1, source_target_pairs={{4,0},{8,4},{12,8},{16,12},{20,16},{24,20},{28,24},{5,1},{9,5},{13... | collective-permute-start | bytes 69128 | tf_op jit(solution)/shard_map/ppermute | solution.py:29
  19.5 3.7 %collective-permute-start = (f32[]{:T(128)}, f32[]{:T(128)}, u32[]{:S(2)}, u32[]{:S(2)}) collective-permute-start(f32[]{:T(128)} %get-tuple-element.536), channel_id=1, source_target_pairs={{0,1},{1,2},{2,3},{3,0},{4,5},{5,6},{6,7},{7,4},{8,9},{9,10},{10,1... | collective-permute-start | bytes 20 | tf_op jit(solution)/shard_map/ppermute | solution.py:40
  24.6 4.5 %collective-permute-start.1 = (f32[]{:T(128)}, f32[]{:T(128)}, u32[]{:S(2)}, u32[]{:S(2)}) collective-permute-start(f32[]{:T(128)} %max.18), channel_id=1, source_target_pairs={{0,2},{1,3},{2,0},{3,1},{4,6},{5,7},{6,4},{7,5},{8,10},{9,11},{10,... | collective-permute-start | bytes 20 | tf_op jit(solution)/shard_map/ppermute | solution.py:40
  29.7 3.0 %collective-permute-start.2 = (f32[]{:T(128)}, f32[]{:T(128)}, u32[]{:S(2)}, u32[]{:S(2)}) collective-permute-start(f32[]{:T(128)} %max.19), channel_id=1, source_target_pairs={{0,4},{4,8},{8,12},{12,16},{16,20},{20,24},{24,28},{28,0},{1,5},{5... | collective-permute-start | bytes 20 | tf_op jit(solution)/shard_map/ppermute | solution.py:40
  33.4 3.9 %collective-permute-start.3 = (f32[]{:T(128)}, f32[]{:T(128)}, u32[]{:S(2)}, u32[]{:S(2)}) collective-permute-start(f32[]{:T(128)} %max.20), channel_id=1, source_target_pairs={{0,8},{4,12},{8,16},{12,20},{16,24},{20,28},{24,0},{28,4},{1,9},{5... | collective-permute-start | bytes 20 | tf_op jit(solution)/shard_map/ppermute | solution.py:40
  38.0 3.6 %collective-permute-start.4 = (f32[]{:T(128)}, f32[]{:T(128)}, u32[]{:S(2)}, u32[]{:S(2)}) collective-permute-start(f32[]{:T(128)} %max.21), channel_id=1, source_target_pairs={{0,16},{4,20},{8,24},{12,28},{16,0},{20,4},{24,8},{28,12},{1,17},{... | collective-permute-start | bytes 20 | tf_op jit(solution)/shard_map/ppermute | solution.py:40
  42.6 4.3 %collective-permute-start.8 = (f32[1,15,224]{2,1,0:T(8,128)S(1)}, f32[1,15,224]{2,1,0:T(8,128)S(1)}, u32[]{:S(2)}, u32[]{:S(2)}) collective-permute-start(f32[1,15,224]{2,1,0:T(8,128)S(1)} %maximum_bitcast_fusion.3), channel_id=1, source_target_pairs={{1,0},{2,1},{3,2},{5,4},{6,5},{7,6},{9,8},{10,9},{11,10},{13,12},{... | collective-permute-start | bytes 40328 | tf_op jit(solution)/shard_map/ppermute | solution.py:29
  45.5 5.6 %collective-permute-start.7 = (f32[1,15,224]{2,1,0:T(8,128)S(1)}, f32[1,15,224]{2,1,0:T(8,128)S(1)}, u32[]{:S(2)}, u32[]{:S(2)}) collective-permute-start(f32[1,15,224]{2,1,0:T(8,128)S(1)} %maximum_bitcast_fusion.2), channel_id=1, source_target_pairs={{0,1},{1,2},{2,3},{4,5},{5,6},{6,7},{8,9},{9,10},{10,11},{12,13},{... | collective-permute-start | bytes 40328 | tf_op jit(solution)/shard_map/ppermute | solution.py:28
  56.9 23.2 %copy-start.5 = (f32[3,2048]{1,0:T(4,128)S(1)}, f32[3,2048]{1,0:T(4,128)}, u32[]{:S(2)}) copy-start(f32[3,2048]{1,0:T(4,128)} %param.37) | copy-start | bytes 73732
  56.9 23.5 %copy-start.1 = (f32[3,2048]{1,0:T(4,128)S(1)}, f32[3,2048]{1,0:T(4,128)}, u32[]{:S(2)}) copy-start(f32[3,2048]{1,0:T(4,128)} %param.40) | copy-start | bytes 73732
  56.9 23.5 %copy-start.3 = (f32[3,2048]{1,0:T(4,128)S(1)}, f32[3,2048]{1,0:T(4,128)}, u32[]{:S(2)}) copy-start(f32[3,2048]{1,0:T(4,128)} %param.39) | copy-start | bytes 73732
  80.1 14.2 %copy-start.2 = (f32[2048]{0:T(1024)S(1)}, f32[2048]{0:T(1024)}, u32[]{:S(2)}) copy-start(f32[2048]{0:T(1024)} %param.42) | copy-start | bytes 24580
  80.2 14.2 %copy-start.6 = (f32[2048]{0:T(1024)S(1)}, f32[2048]{0:T(1024)}, u32[]{:S(2)}) copy-start(f32[2048]{0:T(1024)} %param.41) | copy-start | bytes 24580
  80.3 14.9 %copy-start.4 = (f32[2048]{0:T(1024)S(1)}, f32[2048]{0:T(1024)}, u32[]{:S(2)}) copy-start(f32[2048]{0:T(1024)} %param.38) | copy-start | bytes 24580
  88.0 7.8 %collective-permute-start.9 = (f32[1,3,384]{2,1,0:T(4,128)S(1)}, f32[1,3,384]{2,1,0:T(4,128)S(1)}, u32[]{:S(2)}, u32[]{:S(2)}) collective-permute-start(f32[1,3,384]{2,1,0:T(4,128)S(1)} %maximum_bitcast_fusion.4), channel_id=1, source_target_pairs={{0,4},{4,8},{8,12},{12,16},{16,20},{20,24},{24,28},{1,5},{5,9},{9,... | collective-permute-start | bytes 13832 | tf_op jit(solution)/shard_map/ppermute | solution.py:28
  90.6 5.3 %collective-permute-start.10 = (f32[1,3,384]{2,1,0:T(4,128)S(1)}, f32[1,3,384]{2,1,0:T(4,128)S(1)}, u32[]{:S(2)}, u32[]{:S(2)}) collective-permute-start(f32[1,3,384]{2,1,0:T(4,128)S(1)} %maximum_bitcast_fusion.5), channel_id=1, source_target_pairs={{4,0},{8,4},{12,8},{16,12},{20,16},{24,20},{28,24},{5,1},{9,5},{13... | collective-permute-start | bytes 13832 | tf_op jit(solution)/shard_map/ppermute | solution.py:29
  96.1 3.7 %collective-permute-start.12 = (f32[1,3,224]{2,1,0:T(4,128)S(1)}, f32[1,3,224]{2,1,0:T(4,128)S(1)}, u32[]{:S(2)}, u32[]{:S(2)}) collective-permute-start(f32[1,3,224]{2,1,0:T(4,128)S(1)} %maximum_bitcast_fusion.13), channel_id=1, source_target_pairs={{1,0},{2,1},{3,2},{5,4},{6,5},{7,6},{9,8},{10,9},{11,10},{13,12},{... | collective-permute-start | bytes 8072 | tf_op jit(solution)/shard_map/ppermute | solution.py:29
  98.5 5.5 %collective-permute-start.11 = (f32[1,3,224]{2,1,0:T(4,128)S(1)}, f32[1,3,224]{2,1,0:T(4,128)S(1)}, u32[]{:S(2)}, u32[]{:S(2)}) collective-permute-start(f32[1,3,224]{2,1,0:T(4,128)S(1)} %maximum_bitcast_fusion.12), channel_id=1, source_target_pairs={{0,1},{1,2},{2,3},{4,5},{5,6},{6,7},{8,9},{9,10},{10,11},{12,13},{... | collective-permute-start | bytes 8072 | tf_op jit(solution)/shard_map/ppermute | solution.py:28
  121.6 6.6 %collective-permute-start.13 = (f32[1,3,384]{2,1,0:T(4,128)S(1)}, f32[1,3,384]{2,1,0:T(4,128)S(1)}, u32[]{:S(2)}, u32[]{:S(2)}) collective-permute-start(f32[1,3,384]{2,1,0:T(4,128)S(1)} %maximum_bitcast_fusion.6), channel_id=1, source_target_pairs={{0,4},{4,8},{8,12},{12,16},{16,20},{20,24},{24,28},{1,5},{5,9},{9,... | collective-permute-start | bytes 13832 | tf_op jit(solution)/shard_map/ppermute | solution.py:28
  124.2 5.0 %collective-permute-start.14 = (f32[1,3,384]{2,1,0:T(4,128)S(1)}, f32[1,3,384]{2,1,0:T(4,128)S(1)}, u32[]{:S(2)}, u32[]{:S(2)}) collective-permute-start(f32[1,3,384]{2,1,0:T(4,128)S(1)} %maximum_bitcast_fusion.7), channel_id=1, source_target_pairs={{4,0},{8,4},{12,8},{16,12},{20,16},{24,20},{28,24},{5,1},{9,5},{13... | collective-permute-start | bytes 13832 | tf_op jit(solution)/shard_map/ppermute | solution.py:29
  129.3 5.1 %collective-permute-start.16 = (f32[1,3,224]{2,1,0:T(4,128)S(1)}, f32[1,3,224]{2,1,0:T(4,128)S(1)}, u32[]{:S(2)}, u32[]{:S(2)}) collective-permute-start(f32[1,3,224]{2,1,0:T(4,128)S(1)} %maximum_bitcast_fusion.15), channel_id=1, source_target_pairs={{1,0},{2,1},{3,2},{5,4},{6,5},{7,6},{9,8},{10,9},{11,10},{13,12},{... | collective-permute-start | bytes 8072 | tf_op jit(solution)/shard_map/ppermute | solution.py:29
  133.0 5.5 %collective-permute-start.15 = (f32[1,3,224]{2,1,0:T(4,128)S(1)}, f32[1,3,224]{2,1,0:T(4,128)S(1)}, u32[]{:S(2)}, u32[]{:S(2)}) collective-permute-start(f32[1,3,224]{2,1,0:T(4,128)S(1)} %maximum_bitcast_fusion.14), channel_id=1, source_target_pairs={{0,1},{1,2},{2,3},{4,5},{5,6},{6,7},{8,9},{9,10},{10,11},{12,13},{... | collective-permute-start | bytes 8072 | tf_op jit(solution)/shard_map/ppermute | solution.py:28
  156.0 6.6 %collective-permute-start.17 = (f32[1,3,384]{2,1,0:T(4,128)S(1)}, f32[1,3,384]{2,1,0:T(4,128)S(1)}, u32[]{:S(2)}, u32[]{:S(2)}) collective-permute-start(f32[1,3,384]{2,1,0:T(4,128)S(1)} %maximum_bitcast_fusion.8), channel_id=1, source_target_pairs={{0,4},{4,8},{8,12},{12,16},{16,20},{20,24},{24,28},{1,5},{5,9},{9,... | collective-permute-start | bytes 13832 | tf_op jit(solution)/shard_map/ppermute | solution.py:28
  158.5 5.0 %collective-permute-start.18 = (f32[1,3,384]{2,1,0:T(4,128)S(1)}, f32[1,3,384]{2,1,0:T(4,128)S(1)}, u32[]{:S(2)}, u32[]{:S(2)}) collective-permute-start(f32[1,3,384]{2,1,0:T(4,128)S(1)} %maximum_bitcast_fusion.9), channel_id=1, source_target_pairs={{4,0},{8,4},{12,8},{16,12},{20,16},{24,20},{28,24},{5,1},{9,5},{13... | collective-permute-start | bytes 13832 | tf_op jit(solution)/shard_map/ppermute | solution.py:29
  163.7 3.3 %collective-permute-start.20 = (f32[1,3,224]{2,1,0:T(4,128)S(1)}, f32[1,3,224]{2,1,0:T(4,128)S(1)}, u32[]{:S(2)}, u32[]{:S(2)}) collective-permute-start(f32[1,3,224]{2,1,0:T(4,128)S(1)} %maximum_bitcast_fusion.17), channel_id=1, source_target_pairs={{1,0},{2,1},{3,2},{5,4},{6,5},{7,6},{9,8},{10,9},{11,10},{13,12},{... | collective-permute-start | bytes 8072 | tf_op jit(solution)/shard_map/ppermute | solution.py:29
  165.7 5.5 %collective-permute-start.19 = (f32[1,3,224]{2,1,0:T(4,128)S(1)}, f32[1,3,224]{2,1,0:T(4,128)S(1)}, u32[]{:S(2)}, u32[]{:S(2)}) collective-permute-start(f32[1,3,224]{2,1,0:T(4,128)S(1)} %maximum_bitcast_fusion.16), channel_id=1, source_target_pairs={{0,1},{1,2},{2,3},{4,5},{5,6},{6,7},{8,9},{9,10},{10,11},{12,13},{... | collective-permute-start | bytes 8072 | tf_op jit(solution)/shard_map/ppermute | solution.py:28
  188.6 6.3 %collective-permute-start.21 = (f32[1,3,384]{2,1,0:T(4,128)S(1)}, f32[1,3,384]{2,1,0:T(4,128)S(1)}, u32[]{:S(2)}, u32[]{:S(2)}) collective-permute-start(f32[1,3,384]{2,1,0:T(4,128)S(1)} %maximum_bitcast_fusion.10), channel_id=1, source_target_pairs={{0,4},{4,8},{8,12},{12,16},{16,20},{20,24},{24,28},{1,5},{5,9},{9,... | collective-permute-start | bytes 13832 | tf_op jit(solution)/shard_map/ppermute | solution.py:28
  191.2 5.0 %collective-permute-start.22 = (f32[1,3,384]{2,1,0:T(4,128)S(1)}, f32[1,3,384]{2,1,0:T(4,128)S(1)}, u32[]{:S(2)}, u32[]{:S(2)}) collective-permute-start(f32[1,3,384]{2,1,0:T(4,128)S(1)} %maximum_bitcast_fusion.11), channel_id=1, source_target_pairs={{4,0},{8,4},{12,8},{16,12},{20,16},{24,20},{28,24},{5,1},{9,5},{13... | collective-permute-start | bytes 13832 | tf_op jit(solution)/shard_map/ppermute | solution.py:29
  196.3 3.3 %collective-permute-start.24 = (f32[1,3,224]{2,1,0:T(4,128)S(1)}, f32[1,3,224]{2,1,0:T(4,128)S(1)}, u32[]{:S(2)}, u32[]{:S(2)}) collective-permute-start(f32[1,3,224]{2,1,0:T(4,128)S(1)} %maximum_bitcast_fusion.19), channel_id=1, source_target_pairs={{1,0},{2,1},{3,2},{5,4},{6,5},{7,6},{9,8},{10,9},{11,10},{13,12},{... | collective-permute-start | bytes 8072 | tf_op jit(solution)/shard_map/ppermute | solution.py:29
  198.3 5.5 %collective-permute-start.23 = (f32[1,3,224]{2,1,0:T(4,128)S(1)}, f32[1,3,224]{2,1,0:T(4,128)S(1)}, u32[]{:S(2)}, u32[]{:S(2)}) collective-permute-start(f32[1,3,224]{2,1,0:T(4,128)S(1)} %maximum_bitcast_fusion.18), channel_id=1, source_target_pairs={{0,1},{1,2},{2,3},{4,5},{5,6},{6,7},{8,9},{9,10},{10,11},{12,13},{... | collective-permute-start | bytes 8072 | tf_op jit(solution)/shard_map/ppermute | solution.py:28
  (2 other events, 5.0 us)
where the time goes:
time: 216 us; the launch traced here: 215 us
  starting transfers between devices  54.2 us (25%)
  local copies, waits for them, and re-layouts  51.9 us (24%)
  matrix products  39.3 us (18%)
  waiting for transfers between devices  32.5 us (15%)
  other arithmetic  29.3 us (14%)
  between operations  6.97 us (3%)
    dot_general x10, matrix products, fold_batch(): jnp.einsum('rtb,tab->rta', qsel, weight, precision=lax.Precision.HIGH, pr...  36.7 us
    ppermute x10, starting transfers between devices, extended(): after = lax.ppermute(leading, axis, down)  30.9 us
    gather x40, local copies, waits for them, and re-layouts, spread_ghosts(): jnp.take(rows, ghost_index[starts[d]:starts[d] + sizes[d]], axis=1)  29 us
    ppermute x10, waiting for transfers between devices, extended(): before = lax.ppermute(last, axis, up)  20.7 us
    ppermute x10, starting transfers between devices, extended(): before = lax.ppermute(last, axis, up)  16 us
    ppermute x5, waiting for transfers between devices, mesh_max(): value = jnp.maximum(value, lax.ppermute(value, axis, pairs))  8.83 us
    ppermute x5, starting transfers between devices, mesh_max(): value = jnp.maximum(value, lax.ppermute(value, axis, pairs))  7.3 us
    dynamic_update_slice x2, other arithmetic, hydro_step(): stored = lax.dynamic_update_slice_in_dim(stored, weight, offset, 0)  6.18 us
  transfers between devices with their start and end apart: 25, of which 14 were waited for; matrix products, arithmetic and copies ran while one was open for 5% of the time, Pallas kernels for 0%

commit v1 on v0

--- a/solution.py
+++ b/solution.py
@@ -32,14 +32,9 @@
 
 
 def mesh_max(value):
-    for axis in ("gy", "gx"):
-        size = lax.axis_size(axis)
-        shift = 1
-        while shift < size:
-            pairs = [(i, (i + shift) % size) for i in range(size)]
-            value = jnp.maximum(value, lax.ppermute(value, axis, pairs))
-            shift = shift * 2
-    return value
+    count = lax.axis_size("gx") * lax.axis_size("gy")
+    spread = jnp.full((count, 1), value, jnp.float32)
+    return jnp.max(lax.all_to_all(spread, ("gx", "gy"), 0, 0, tiled=True))
 
 
 def ghost_sizes():

time: 216 us -> 211 us (0.977)
  the two profiles are of different devices: /device:TPU:30 before, /device:TPU:20 now
where the time goes in v1:
time: 211 us; the launch traced here: 209 us
  starting transfers between devices  66.4 us (31%)
  local copies, waits for them, and re-layouts  53.2 us (25%)
  matrix products  39.3 us (19%)
  other arithmetic  30 us (14%)
  waiting for transfers between devices  13.5 us (6%)
  between operations  5.45 us (3%)
    dot_general x10, matrix products, fold_batch(): jnp.einsum('rtb,tab->rta', qsel, weight, precision=lax.Precision.HIGH, pr...  36.7 us
    ppermute x10, starting transfers between devices, extended(): after = lax.ppermute(leading, axis, down)  33.7 us
    gather x40, local copies, waits for them, and re-layouts, spread_ghosts(): jnp.take(rows, ghost_index[starts[d]:starts[d] + sizes[d]], axis=1)  29 us
    ppermute x10, starting transfers between devices, extended(): before = lax.ppermute(last, axis, up)  27.8 us
    ppermute x10, waiting for transfers between devices, extended(): before = lax.ppermute(last, axis, up)  9.01 us
    dynamic_update_slice x2, other arithmetic, hydro_step(): stored = lax.dynamic_update_slice_in_dim(stored, weight, offset, 0)  6.18 us
    gather x10, local copies, waits for them, and re-layouts, fold_batch(): qsel = jnp.take(blocks, far_ids, axis=1)  5.9 us
    and x8, other arithmetic, fold_batch(): qsel = jnp.take(blocks, far_ids, axis=1)  5.82 us
  transfers between devices with their start and end apart: 21, of which 9 were waited for; matrix products, arithmetic and copies ran while one was open for 6% of the time, Pallas kernels for 0%

profile of v1, /device:TPU:20, one launch (start us, length us, event | category | flops | bytes accessed | tf_op | source)
XLA Modules:
  0.0 208.6 jit_solution(15003506733310205715)
XLA Ops:
  15.9 4.5 %collective-permute-start.1 = (f32[1,15,384]{2,1,0:T(8,128)S(1)}, f32[1,15,384]{2,1,0:T(8,128)S(1)}, u32[]{:S(2)}, u32[]{:S(2)}) collective-permute-start(f32[1,15,384]{2,1,0:T(8,128)S(1)} %maximum_bitcast_fusion.1), channel_id=1, source_target_pairs={{4,0},{8,4},{12,8},{16,12},{20,16},{24,20},{28,24},{5,1},{9,5},{13... | collective-permute-start | bytes 69128 | tf_op jit(solution)/shard_map/ppermute | solution.py:29
  21.7 5.0 %all-to-all-start = ((f32[32,1,1]{2,1,0:T(1,128)}), f32[32,1,1]{2,1,0:T(1,128)S(1)}, u32[]{:S(2)}, u32[]{:S(2)}) async-start(f32[32,1,1]{2,1,0:T(1,128)} %broadcast_in_dim.155), calls=%async_computation | async-start | bytes 32768 | tf_op jit(solution)/shard_map/all_to_all | solution.py:37
  34.3 3.3 %collective-permute-start.3 = (f32[1,15,224]{2,1,0:T(8,128)S(1)}, f32[1,15,224]{2,1,0:T(8,128)S(1)}, u32[]{:S(2)}, u32[]{:S(2)}) collective-permute-start(f32[1,15,224]{2,1,0:T(8,128)S(1)} %maximum_bitcast_fusion.3), channel_id=1, source_target_pairs={{1,0},{2,1},{3,2},{5,4},{6,5},{7,6},{9,8},{10,9},{11,10},{13,12},{... | collective-permute-start | bytes 40328 | tf_op jit(solution)/shard_map/ppermute | solution.py:29
  37.7 2.5 %collective-permute-start.2 = (f32[1,15,224]{2,1,0:T(8,128)S(1)}, f32[1,15,224]{2,1,0:T(8,128)S(1)}, u32[]{:S(2)}, u32[]{:S(2)}) collective-permute-start(f32[1,15,224]{2,1,0:T(8,128)S(1)} %maximum_bitcast_fusion.2), channel_id=1, source_target_pairs={{0,1},{1,2},{2,3},{4,5},{5,6},{6,7},{8,9},{9,10},{10,11},{12,13},{... | collective-permute-start | bytes 40328 | tf_op jit(solution)/shard_map/ppermute | solution.py:28
  40.3 3.0 %collective-permute-done.2 = f32[1,15,224]{2,1,0:T(8,128)S(1)} collective-permute-done((f32[1,15,224]{2,1,0:T(8,128)S(1)}, f32[1,15,224]{2,1,0:T(8,128)S(1)}, u32[]{:S(2)}, u32[]{:S(2)}) %collective-permute-start.2) | collective-permute-done | bytes 13472 | tf_op jit(solution)/shard_map/ppermute | solution.py:28
  46.6 2.4 %broadcast_in_dim.157 = f32[64,128,128]{2,1,0:T(8,128)} broadcast(f32[]{:T(128)} %constant.71.clone.1), dimensions={} | broadcast | bytes 4194308 | tf_op jit(solution)/shard_map/broadcast_in_dim | solution.py:244
  49.1 23.1 %while.57 = (s32[]{:T(128)}, f32[53,16,128]{2,1,0:T(8,128)S(1)}, f32[64,128,128]{2,1,0:T(8,128)}, s32[]{:T(128)}, s32[64]{0:T(128)S(1)}, /*index=5*/f32[3,25,128...) while((s32[]{:T(128)}, f32[53,16,128]{2,1,0:T(8,128)S(1)}, ...), condition=%wide.region_5.10_spmd.clone, body=%wide.region_4.9_spmd.clone.sunk | while | flops 221341216 | bytes 8103835 | solution.py:245
  50.8 3.1 %fusion.223 = f32[64,128,128]{2,1,0:T(8,128)} fusion(f32[64,128,128]{2,1,0:T(8,128)} %get-tuple-element.1074, s32[]{:T(128)S(6)} %select_n.425, f32[32,128]{1,0:T(8,128)S(1)} %bitcast.552, f32[32,128]{1,0:T(8,128)S(1)} %bitcast.558, f32[32,128]{1,0:T(8,128)S(1)} %bitcast.554, f32[32,128]{1,0:T(8,128)S(1)} %bitcast.560, f32[32,128]{1,0:T(8,128)S(1)} %bitcast.550, ...), kind=kLoop, calls=%fused_computation.53.clone.1 | loop fusion | flops 6291456 | bytes 2195460 | tf_op jit(solution)/shard_map/while/body/dynamic_update_slice | solution.py:240
  54.5 4.9 %fusion.221 = f32[53,32,128]{2,0,1:T(8,128)S(1)} fusion(f32[32,128]{1,0:T(8,128)S(1)} %bitcast.553, f32[32,128]{1,0:T(8,128)S(1)} %bitcast.559, f32[32,128]{1,0:T(8,128)S(1)} %bitcast.555, f32[32,128]{1,0:T(8,128)S(1)} %bitcast.561, f32[32,128]{1,0:T(8,128)S(1)} %bitcast.551, f32[32,128]{1,0:T(8,128)S(1)} %bitcast.557, ...), kind=kOutput, calls=%fused_computation.55.clone.1 | convolution fusion | flops 173232128 | bytes 1835040 | tf_op jit(solution)/shard_map/while/body/rtb,tab->rta/dot_general | solution.py:218
  62.3 3.1 %fusion.223 = f32[64,128,128]{2,1,0:T(8,128)} fusion(f32[64,128,128]{2,1,0:T(8,128)} %get-tuple-element.1074, s32[]{:T(128)S(6)} %select_n.425, f32[32,128]{1,0:T(8,128)S(1)} %bitcast.552, f32[32,128]{1,0:T(8,128)S(1)} %bitcast.558, f32[32,128]{1,0:T(8,128)S(1)} %bitcast.554, f32[32,128]{1,0:T(8,128)S(1)} %bitcast.560, f32[32,128]{1,0:T(8,128)S(1)} %bitcast.550, ...), kind=kLoop, calls=%fused_computation.53.clone.1 | loop fusion | flops 6291456 | bytes 2195460 | tf_op jit(solution)/shard_map/while/body/dynamic_update_slice | solution.py:240
  66.0 4.9 %fusion.221 = f32[53,32,128]{2,0,1:T(8,128)S(1)} fusion(f32[32,128]{1,0:T(8,128)S(1)} %bitcast.553, f32[32,128]{1,0:T(8,128)S(1)} %bitcast.559, f32[32,128]{1,0:T(8,128)S(1)} %bitcast.555, f32[32,128]{1,0:T(8,128)S(1)} %bitcast.561, f32[32,128]{1,0:T(8,128)S(1)} %bitcast.551, f32[32,128]{1,0:T(8,128)S(1)} %bitcast.557, ...), kind=kOutput, calls=%fused_computation.55.clone.1 | convolution fusion | flops 173232128 | bytes 1835040 | tf_op jit(solution)/shard_map/while/body/rtb,tab->rta/dot_general | solution.py:218
  82.8 4.5 %collective-permute-start.5 = (f32[1,3,384]{2,1,0:T(4,128)S(1)}, f32[1,3,384]{2,1,0:T(4,128)S(1)}, u32[]{:S(2)}, u32[]{:S(2)}) collective-permute-start(f32[1,3,384]{2,1,0:T(4,128)S(1)} %maximum_bitcast_fusion.5), channel_id=1, source_target_pairs={{4,0},{8,4},{12,8},{16,12},{20,16},{24,20},{28,24},{5,1},{9,5},{13... | collective-permute-start | bytes 13832 | tf_op jit(solution)/shard_map/ppermute | solution.py:29
  91.1 3.9 %collective-permute-start.6 = (f32[1,3,224]{2,1,0:T(4,128)S(1)}, f32[1,3,224]{2,1,0:T(4,128)S(1)}, u32[]{:S(2)}, u32[]{:S(2)}) collective-permute-start(f32[1,3,224]{2,1,0:T(4,128)S(1)} %maximum_bitcast_fusion.12), channel_id=1, source_target_pairs={{0,1},{1,2},{2,3},{4,5},{5,6},{6,7},{8,9},{9,10},{10,11},{12,13},{... | collective-permute-start | bytes 8072 | tf_op jit(solution)/shard_map/ppermute | solution.py:28
  97.2 10.2 %while.58 = (s32[]{:T(128)}, f32[7,16,128]{2,1,0:T(8,128)S(1)}, s32[]{:T(128)}, f32[64,128,128]{2,1,0:T(8,128)}, s32[64]{0:T(128)S(1)}, /*index=5*/f32[7,25,128]...) while((s32[]{:T(128)}, f32[7,16,128]{2,1,0:T(8,128)S(1)}, ...), condition=%wide.region_9.18_spmd.clone, body=%wide.region_8.0_spmd.clone.sunk | while | flops 27570436 | bytes 2790583 | solution.py:268
  98.8 3.4 %fusion.228 = f32[7,32,128]{2,0,1:T(8,128)S(1)} fusion(f32[64,128,128]{2,1,0:T(8,128)} %get-tuple-element.1125, s32[]{:T(128)S(6)} %select_n.427, f32[32,7,128]{2,1,0:T(8,128)S(1)} %gather_fusion.3, pred[32]{0:T(512)(128)(4,1)S(1)} %get-tuple-element.1024), kind=kOutput, calls=%fused_computation.92.clone.1 | convolution fusion | flops 22048768 | bytes 2326564 | tf_op jit(solution)/shard_map/while/body/rtb,tab->rta/dot_general | solution.py:218
  103.7 3.4 %fusion.228 = f32[7,32,128]{2,0,1:T(8,128)S(1)} fusion(f32[64,128,128]{2,1,0:T(8,128)} %get-tuple-element.1125, s32[]{:T(128)S(6)} %select_n.427, f32[32,7,128]{2,1,0:T(8,128)S(1)} %gather_fusion.3, pred[32]{0:T(512)(128)(4,1)S(1)} %get-tuple-element.1024), kind=kOutput, calls=%fused_computation.92.clone.1 | convolution fusion | flops 22048768 | bytes 2326564 | tf_op jit(solution)/shard_map/while/body/rtb,tab->rta/dot_general | solution.py:218
  116.8 4.5 %collective-permute-start.9 = (f32[1,3,384]{2,1,0:T(4,128)S(1)}, f32[1,3,384]{2,1,0:T(4,128)S(1)}, u32[]{:S(2)}, u32[]{:S(2)}) collective-permute-start(f32[1,3,384]{2,1,0:T(4,128)S(1)} %maximum_bitcast_fusion.7), channel_id=1, source_target_pairs={{4,0},{8,4},{12,8},{16,12},{20,16},{24,20},{28,24},{5,1},{9,5},{13... | collective-permute-start | bytes 13832 | tf_op jit(solution)/shard_map/ppermute | solution.py:29
  124.8 3.9 %collective-permute-start.10 = (f32[1,3,224]{2,1,0:T(4,128)S(1)}, f32[1,3,224]{2,1,0:T(4,128)S(1)}, u32[]{:S(2)}, u32[]{:S(2)}) collective-permute-start(f32[1,3,224]{2,1,0:T(4,128)S(1)} %maximum_bitcast_fusion.14), channel_id=1, source_target_pairs={{0,1},{1,2},{2,3},{4,5},{5,6},{6,7},{8,9},{9,10},{10,11},{12,13},{... | collective-permute-start | bytes 8072 | tf_op jit(solution)/shard_map/ppermute | solution.py:28
  130.9 10.0 %while.59 = (s32[]{:T(128)}, f32[7,16,128]{2,1,0:T(8,128)S(1)}, s32[]{:T(128)}, f32[64,128,128]{2,1,0:T(8,128)}, s32[64]{0:T(128)S(1)}, /*index=5*/f32[7,25,128]...) while((s32[]{:T(128)}, f32[7,16,128]{2,1,0:T(8,128)S(1)}, ...), condition=%wide.region_13.22_spmd.clone, body=%wide.region_12.21_spmd.clone.sunk | while | flops 27570436 | bytes 2790583 | solution.py:268
  132.2 3.4 %fusion.234 = f32[7,32,128]{2,0,1:T(8,128)S(1)} fusion(f32[64,128,128]{2,1,0:T(8,128)} %get-tuple-element.1161, s32[]{:T(128)S(6)} %select_n.429, f32[32,7,128]{2,1,0:T(8,128)S(1)} %gather_fusion.4, pred[32]{0:T(512)(128)(4,1)S(1)} %get-tuple-element.1035), kind=kOutput, calls=%fused_computation.113.clone.1 | convolution fusion | flops 22048768 | bytes 2326564 | tf_op jit(solution)/shard_map/while/body/rtb,tab->rta/dot_general | solution.py:218
  137.2 3.4 %fusion.234 = f32[7,32,128]{2,0,1:T(8,128)S(1)} fusion(f32[64,128,128]{2,1,0:T(8,128)} %get-tuple-element.1161, s32[]{:T(128)S(6)} %select_n.429, f32[32,7,128]{2,1,0:T(8,128)S(1)} %gather_fusion.4, pred[32]{0:T(512)(128)(4,1)S(1)} %get-tuple-element.1035), kind=kOutput, calls=%fused_computation.113.clone.1 | convolution fusion | flops 22048768 | bytes 2326564 | tf_op jit(solution)/shard_map/while/body/rtb,tab->rta/dot_general | solution.py:218
  150.3 4.5 %collective-permute-start.13 = (f32[1,3,384]{2,1,0:T(4,128)S(1)}, f32[1,3,384]{2,1,0:T(4,128)S(1)}, u32[]{:S(2)}, u32[]{:S(2)}) collective-permute-start(f32[1,3,384]{2,1,0:T(4,128)S(1)} %maximum_bitcast_fusion.9), channel_id=1, source_target_pairs={{4,0},{8,4},{12,8},{16,12},{20,16},{24,20},{28,24},{5,1},{9,5},{13... | collective-permute-start | bytes 13832 | tf_op jit(solution)/shard_map/ppermute | solution.py:29
  158.4 3.9 %collective-permute-start.14 = (f32[1,3,224]{2,1,0:T(4,128)S(1)}, f32[1,3,224]{2,1,0:T(4,128)S(1)}, u32[]{:S(2)}, u32[]{:S(2)}) collective-permute-start(f32[1,3,224]{2,1,0:T(4,128)S(1)} %maximum_bitcast_fusion.16), channel_id=1, source_target_pairs={{0,1},{1,2},{2,3},{4,5},{5,6},{6,7},{8,9},{9,10},{10,11},{12,13},{... | collective-permute-start | bytes 8072 | tf_op jit(solution)/shard_map/ppermute | solution.py:28
  164.4 10.0 %while.60 = (s32[]{:T(128)}, f32[7,16,128]{2,1,0:T(8,128)S(1)}, s32[]{:T(128)}, f32[64,128,128]{2,1,0:T(8,128)}, s32[64]{0:T(128)S(1)}, /*index=5*/f32[7,25,128]...) while((s32[]{:T(128)}, f32[7,16,128]{2,1,0:T(8,128)S(1)}, ...), condition=%wide.region_17.26_spmd.clone, body=%wide.region_16.25_spmd.clone.sunk | while | flops 27570436 | bytes 2790583 | solution.py:268
  165.8 3.4 %fusion.240 = f32[7,32,128]{2,0,1:T(8,128)S(1)} fusion(f32[64,128,128]{2,1,0:T(8,128)} %get-tuple-element.1197, s32[]{:T(128)S(6)} %select_n.431, f32[32,7,128]{2,1,0:T(8,128)S(1)} %gather_fusion.5, pred[32]{0:T(512)(128)(4,1)S(1)} %get-tuple-element.1046), kind=kOutput, calls=%fused_computation.134.clone.1 | convolution fusion | flops 22048768 | bytes 2326564 | tf_op jit(solution)/shard_map/while/body/rtb,tab->rta/dot_general | solution.py:218
  170.8 3.4 %fusion.240 = f32[7,32,128]{2,0,1:T(8,128)S(1)} fusion(f32[64,128,128]{2,1,0:T(8,128)} %get-tuple-element.1197, s32[]{:T(128)S(6)} %select_n.431, f32[32,7,128]{2,1,0:T(8,128)S(1)} %gather_fusion.5, pred[32]{0:T(512)(128)(4,1)S(1)} %get-tuple-element.1046), kind=kOutput, calls=%fused_computation.134.clone.1 | convolution fusion | flops 22048768 | bytes 2326564 | tf_op jit(solution)/shard_map/while/body/rtb,tab->rta/dot_general | solution.py:218
  181.3 1.9 collective-permute-start.16
  183.9 4.5 %collective-permute-start.17 = (f32[1,3,384]{2,1,0:T(4,128)S(1)}, f32[1,3,384]{2,1,0:T(4,128)S(1)}, u32[]{:S(2)}, u32[]{:S(2)}) collective-permute-start(f32[1,3,384]{2,1,0:T(4,128)S(1)} %maximum_bitcast_fusion.11), channel_id=1, source_target_pairs={{4,0},{8,4},{12,8},{16,12},{20,16},{24,20},{28,24},{5,1},{9,5},{13... | collective-permute-start | bytes 13832 | tf_op jit(solution)/shard_map/ppermute | solution.py:29
  191.9 3.9 %collective-permute-start.18 = (f32[1,3,224]{2,1,0:T(4,128)S(1)}, f32[1,3,224]{2,1,0:T(4,128)S(1)}, u32[]{:S(2)}, u32[]{:S(2)}) collective-permute-start(f32[1,3,224]{2,1,0:T(4,128)S(1)} %maximum_bitcast_fusion.18), channel_id=1, source_target_pairs={{0,1},{1,2},{2,3},{4,5},{5,6},{6,7},{8,9},{9,10},{10,11},{12,13},{... | collective-permute-start | bytes 8072 | tf_op jit(solution)/shard_map/ppermute | solution.py:28
  197.9 10.0 %while.61 = (s32[]{:T(128)}, f32[7,16,128]{2,1,0:T(8,128)S(1)}, s32[]{:T(128)}, f32[64,128,128]{2,1,0:T(8,128)}, s32[64]{0:T(128)S(1)}, /*index=5*/f32[7,25,128]...) while((s32[]{:T(128)}, f32[7,16,128]{2,1,0:T(8,128)S(1)}, ...), condition=%wide.region_21.30_spmd.clone, body=%wide.region_20.29_spmd.clone.sunk | while | flops 27570436 | bytes 2790583 | solution.py:268
  199.3 3.4 %fusion.246 = f32[7,32,128]{2,0,1:T(8,128)S(1)} fusion(f32[64,128,128]{2,1,0:T(8,128)} %get-tuple-element.1233, s32[]{:T(128)S(6)} %select_n.433, f32[32,7,128]{2,1,0:T(8,128)S(1)} %gather_fusion.6, pred[32]{0:T(512)(128)(4,1)S(1)} %get-tuple-element.1057), kind=kOutput, calls=%fused_computation.155.clone.1 | convolution fusion | flops 22048768 | bytes 2326564 | tf_op jit(solution)/shard_map/while/body/rtb,tab->rta/dot_general | solution.py:218
  204.3 3.4 %fusion.246 = f32[7,32,128]{2,0,1:T(8,128)S(1)} fusion(f32[64,128,128]{2,1,0:T(8,128)} %get-tuple-element.1233, s32[]{:T(128)S(6)} %select_n.433, f32[32,7,128]{2,1,0:T(8,128)S(1)} %gather_fusion.6, pred[32]{0:T(512)(128)(4,1)S(1)} %get-tuple-element.1057), kind=kOutput, calls=%fused_computation.155.clone.1 | convolution fusion | flops 22048768 | bytes 2326564 | tf_op jit(solution)/shard_map/while/body/rtb,tab->rta/dot_general | solution.py:218
  (414 shorter events, 103.0 us)
Async XLA Ops:
  0.6 26.0 %copy-start.7 = (s32[1088]{0:T(1024)S(1)}, s32[1088]{0:T(1024)}, u32[]{:S(2)}) copy-start(s32[1088]{0:T(1024)} %param.44) | copy-start | bytes 13060
  11.0 23.0 %collective-permute-start = (f32[1,15,384]{2,1,0:T(8,128)S(1)}, f32[1,15,384]{2,1,0:T(8,128)S(1)}, u32[]{:S(2)}, u32[]{:S(2)}) collective-permute-start(f32[1,15,384]{2,1,0:T(8,128)S(1)} %maximum_bitcast_fusion), channel_id=1, source_target_pairs={{0,4},{4,8},{8,12},{12,16},{16,20},{20,24},{24,28},{1,5},{5,9},{9,... | collective-permute-start | bytes 69128 | tf_op jit(solution)/shard_map/ppermute | solution.py:28
  15.9 18.3 %collective-permute-start.1 = (f32[1,15,384]{2,1,0:T(8,128)S(1)}, f32[1,15,384]{2,1,0:T(8,128)S(1)}, u32[]{:S(2)}, u32[]{:S(2)}) collective-permute-start(f32[1,15,384]{2,1,0:T(8,128)S(1)} %maximum_bitcast_fusion.1), channel_id=1, source_target_pairs={{4,0},{8,4},{12,8},{16,12},{20,16},{24,20},{28,24},{5,1},{9,5},{13... | collective-permute-start | bytes 69128 | tf_op jit(solution)/shard_map/ppermute | solution.py:29
  21.7 9.1 %all-to-all-start = ((f32[32,1,1]{2,1,0:T(1,128)}), f32[32,1,1]{2,1,0:T(1,128)S(1)}, u32[]{:S(2)}, u32[]{:S(2)}) async-start(f32[32,1,1]{2,1,0:T(1,128)} %broadcast_in_dim.155), calls=%async_computation | async-start | bytes 32768 | tf_op jit(solution)/shard_map/all_to_all | solution.py:37
  34.3 5.9 %collective-permute-start.3 = (f32[1,15,224]{2,1,0:T(8,128)S(1)}, f32[1,15,224]{2,1,0:T(8,128)S(1)}, u32[]{:S(2)}, u32[]{:S(2)}) collective-permute-start(f32[1,15,224]{2,1,0:T(8,128)S(1)} %maximum_bitcast_fusion.3), channel_id=1, source_target_pairs={{1,0},{2,1},{3,2},{5,4},{6,5},{7,6},{9,8},{10,9},{11,10},{13,12},{... | collective-permute-start | bytes 40328 | tf_op jit(solution)/shard_map/ppermute | solution.py:29
  37.7 5.6 %collective-permute-start.2 = (f32[1,15,224]{2,1,0:T(8,128)S(1)}, f32[1,15,224]{2,1,0:T(8,128)S(1)}, u32[]{:S(2)}, u32[]{:S(2)}) collective-permute-start(f32[1,15,224]{2,1,0:T(8,128)S(1)} %maximum_bitcast_fusion.2), channel_id=1, source_target_pairs={{0,1},{1,2},{2,3},{4,5},{5,6},{6,7},{8,9},{9,10},{10,11},{12,13},{... | collective-permute-start | bytes 40328 | tf_op jit(solution)/shard_map/ppermute | solution.py:28
  46.6 2.5 %copy-start = (s32[64]{0:T(128)S(1)}, s32[64]{0:T(128)}, u32[]{:S(2)}) copy-start(s32[64]{0:T(128)} %param.46) | copy-start | bytes 772
  46.6 2.5 %copy-start.8 = (s32[64]{0:T(128)S(1)}, s32[64]{0:T(128)}, u32[]{:S(2)}) copy-start(s32[64]{0:T(128)} %param.45) | copy-start | bytes 772
  49.1 23.2 %copy-start.5 = (f32[3,2048]{1,0:T(4,128)S(1)}, f32[3,2048]{1,0:T(4,128)}, u32[]{:S(2)}) copy-start(f32[3,2048]{1,0:T(4,128)} %param.37) | copy-start | bytes 73732
  49.1 23.5 %copy-start.1 = (f32[3,2048]{1,0:T(4,128)S(1)}, f32[3,2048]{1,0:T(4,128)}, u32[]{:S(2)}) copy-start(f32[3,2048]{1,0:T(4,128)} %param.40) | copy-start | bytes 73732
  49.1 23.5 %copy-start.3 = (f32[3,2048]{1,0:T(4,128)S(1)}, f32[3,2048]{1,0:T(4,128)}, u32[]{:S(2)}) copy-start(f32[3,2048]{1,0:T(4,128)} %param.39) | copy-start | bytes 73732
  72.3 15.1 %copy-start.2 = (f32[2048]{0:T(1024)S(1)}, f32[2048]{0:T(1024)}, u32[]{:S(2)}) copy-start(f32[2048]{0:T(1024)} %param.42) | copy-start | bytes 24580
  72.3 15.1 %copy-start.6 = (f32[2048]{0:T(1024)S(1)}, f32[2048]{0:T(1024)}, u32[]{:S(2)}) copy-start(f32[2048]{0:T(1024)} %param.41) | copy-start | bytes 24580
  72.5 15.8 %copy-start.4 = (f32[2048]{0:T(1024)S(1)}, f32[2048]{0:T(1024)}, u32[]{:S(2)}) copy-start(f32[2048]{0:T(1024)} %param.38) | copy-start | bytes 24580
  80.2 8.7 %collective-permute-start.4 = (f32[1,3,384]{2,1,0:T(4,128)S(1)}, f32[1,3,384]{2,1,0:T(4,128)S(1)}, u32[]{:S(2)}, u32[]{:S(2)}) collective-permute-start(f32[1,3,384]{2,1,0:T(4,128)S(1)} %maximum_bitcast_fusion.4), channel_id=1, source_target_pairs={{0,4},{4,8},{8,12},{12,16},{16,20},{20,24},{24,28},{1,5},{5,9},{9,... | collective-permute-start | bytes 13832 | tf_op jit(solution)/shard_map/ppermute | solution.py:28
  82.8 6.2 %collective-permute-start.5 = (f32[1,3,384]{2,1,0:T(4,128)S(1)}, f32[1,3,384]{2,1,0:T(4,128)S(1)}, u32[]{:S(2)}, u32[]{:S(2)}) collective-permute-start(f32[1,3,384]{2,1,0:T(4,128)S(1)} %maximum_bitcast_fusion.5), channel_id=1, source_target_pairs={{4,0},{8,4},{12,8},{16,12},{20,16},{24,20},{28,24},{5,1},{9,5},{13... | collective-permute-start | bytes 13832 | tf_op jit(solution)/shard_map/ppermute | solution.py:29
  89.1 5.9 %collective-permute-start.7 = (f32[1,3,224]{2,1,0:T(4,128)S(1)}, f32[1,3,224]{2,1,0:T(4,128)S(1)}, u32[]{:S(2)}, u32[]{:S(2)}) collective-permute-start(f32[1,3,224]{2,1,0:T(4,128)S(1)} %maximum_bitcast_fusion.13), channel_id=1, source_target_pairs={{1,0},{2,1},{3,2},{5,4},{6,5},{7,6},{9,8},{10,9},{11,10},{13,12},{... | collective-permute-start | bytes 8072 | tf_op jit(solution)/shard_map/ppermute | solution.py:29
  91.1 5.5 %collective-permute-start.6 = (f32[1,3,224]{2,1,0:T(4,128)S(1)}, f32[1,3,224]{2,1,0:T(4,128)S(1)}, u32[]{:S(2)}, u32[]{:S(2)}) collective-permute-start(f32[1,3,224]{2,1,0:T(4,128)S(1)} %maximum_bitcast_fusion.12), channel_id=1, source_target_pairs={{0,1},{1,2},{2,3},{4,5},{5,6},{6,7},{8,9},{9,10},{10,11},{12,13},{... | collective-permute-start | bytes 8072 | tf_op jit(solution)/shard_map/ppermute | solution.py:28
  114.3 7.5 %collective-permute-start.8 = (f32[1,3,384]{2,1,0:T(4,128)S(1)}, f32[1,3,384]{2,1,0:T(4,128)S(1)}, u32[]{:S(2)}, u32[]{:S(2)}) collective-permute-start(f32[1,3,384]{2,1,0:T(4,128)S(1)} %maximum_bitcast_fusion.6), channel_id=1, source_target_pairs={{0,4},{4,8},{8,12},{12,16},{16,20},{20,24},{24,28},{1,5},{5,9},{9,... | collective-permute-start | bytes 13832 | tf_op jit(solution)/shard_map/ppermute | solution.py:28
  116.8 5.9 %collective-permute-start.9 = (f32[1,3,384]{2,1,0:T(4,128)S(1)}, f32[1,3,384]{2,1,0:T(4,128)S(1)}, u32[]{:S(2)}, u32[]{:S(2)}) collective-permute-start(f32[1,3,384]{2,1,0:T(4,128)S(1)} %maximum_bitcast_fusion.7), channel_id=1, source_target_pairs={{4,0},{8,4},{12,8},{16,12},{20,16},{24,20},{28,24},{5,1},{9,5},{13... | collective-permute-start | bytes 13832 | tf_op jit(solution)/shard_map/ppermute | solution.py:29
  122.8 5.9 %collective-permute-start.11 = (f32[1,3,224]{2,1,0:T(4,128)S(1)}, f32[1,3,224]{2,1,0:T(4,128)S(1)}, u32[]{:S(2)}, u32[]{:S(2)}) collective-permute-start(f32[1,3,224]{2,1,0:T(4,128)S(1)} %maximum_bitcast_fusion.15), channel_id=1, source_target_pairs={{1,0},{2,1},{3,2},{5,4},{6,5},{7,6},{9,8},{10,9},{11,10},{13,12},{... | collective-permute-start | bytes 8072 | tf_op jit(solution)/shard_map/ppermute | solution.py:29
  124.8 5.5 %collective-permute-start.10 = (f32[1,3,224]{2,1,0:T(4,128)S(1)}, f32[1,3,224]{2,1,0:T(4,128)S(1)}, u32[]{:S(2)}, u32[]{:S(2)}) collective-permute-start(f32[1,3,224]{2,1,0:T(4,128)S(1)} %maximum_bitcast_fusion.14), channel_id=1, source_target_pairs={{0,1},{1,2},{2,3},{4,5},{5,6},{6,7},{8,9},{9,10},{10,11},{12,13},{... | collective-permute-start | bytes 8072 | tf_op jit(solution)/shard_map/ppermute | solution.py:28
  147.8 7.5 %collective-permute-start.12 = (f32[1,3,384]{2,1,0:T(4,128)S(1)}, f32[1,3,384]{2,1,0:T(4,128)S(1)}, u32[]{:S(2)}, u32[]{:S(2)}) collective-permute-start(f32[1,3,384]{2,1,0:T(4,128)S(1)} %maximum_bitcast_fusion.8), channel_id=1, source_target_pairs={{0,4},{4,8},{8,12},{12,16},{16,20},{20,24},{24,28},{1,5},{5,9},{9,... | collective-permute-start | bytes 13832 | tf_op jit(solution)/shard_map/ppermute | solution.py:28
  150.3 5.9 %collective-permute-start.13 = (f32[1,3,384]{2,1,0:T(4,128)S(1)}, f32[1,3,384]{2,1,0:T(4,128)S(1)}, u32[]{:S(2)}, u32[]{:S(2)}) collective-permute-start(f32[1,3,384]{2,1,0:T(4,128)S(1)} %maximum_bitcast_fusion.9), channel_id=1, source_target_pairs={{4,0},{8,4},{12,8},{16,12},{20,16},{24,20},{28,24},{5,1},{9,5},{13... | collective-permute-start | bytes 13832 | tf_op jit(solution)/shard_map/ppermute | solution.py:29
  156.4 5.9 %collective-permute-start.15 = (f32[1,3,224]{2,1,0:T(4,128)S(1)}, f32[1,3,224]{2,1,0:T(4,128)S(1)}, u32[]{:S(2)}, u32[]{:S(2)}) collective-permute-start(f32[1,3,224]{2,1,0:T(4,128)S(1)} %maximum_bitcast_fusion.17), channel_id=1, source_target_pairs={{1,0},{2,1},{3,2},{5,4},{6,5},{7,6},{9,8},{10,9},{11,10},{13,12},{... | collective-permute-start | bytes 8072 | tf_op jit(solution)/shard_map/ppermute | solution.py:29
  158.4 5.5 %collective-permute-start.14 = (f32[1,3,224]{2,1,0:T(4,128)S(1)}, f32[1,3,224]{2,1,0:T(4,128)S(1)}, u32[]{:S(2)}, u32[]{:S(2)}) collective-permute-start(f32[1,3,224]{2,1,0:T(4,128)S(1)} %maximum_bitcast_fusion.16), channel_id=1, source_target_pairs={{0,1},{1,2},{2,3},{4,5},{5,6},{6,7},{8,9},{9,10},{10,11},{12,13},{... | collective-permute-start | bytes 8072 | tf_op jit(solution)/shard_map/ppermute | solution.py:28
  181.3 7.2 %collective-permute-start.16 = (f32[1,3,384]{2,1,0:T(4,128)S(1)}, f32[1,3,384]{2,1,0:T(4,128)S(1)}, u32[]{:S(2)}, u32[]{:S(2)}) collective-permute-start(f32[1,3,384]{2,1,0:T(4,128)S(1)} %maximum_bitcast_fusion.10), channel_id=1, source_target_pairs={{0,4},{4,8},{8,12},{12,16},{16,20},{20,24},{24,28},{1,5},{5,9},{9,... | collective-permute-start | bytes 13832 | tf_op jit(solution)/shard_map/ppermute | solution.py:28
  183.9 5.9 %collective-permute-start.17 = (f32[1,3,384]{2,1,0:T(4,128)S(1)}, f32[1,3,384]{2,1,0:T(4,128)S(1)}, u32[]{:S(2)}, u32[]{:S(2)}) collective-permute-start(f32[1,3,384]{2,1,0:T(4,128)S(1)} %maximum_bitcast_fusion.11), channel_id=1, source_target_pairs={{4,0},{8,4},{12,8},{16,12},{20,16},{24,20},{28,24},{5,1},{9,5},{13... | collective-permute-start | bytes 13832 | tf_op jit(solution)/shard_map/ppermute | solution.py:29
  189.9 5.9 %collective-permute-start.19 = (f32[1,3,224]{2,1,0:T(4,128)S(1)}, f32[1,3,224]{2,1,0:T(4,128)S(1)}, u32[]{:S(2)}, u32[]{:S(2)}) collective-permute-start(f32[1,3,224]{2,1,0:T(4,128)S(1)} %maximum_bitcast_fusion.19), channel_id=1, source_target_pairs={{1,0},{2,1},{3,2},{5,4},{6,5},{7,6},{9,8},{10,9},{11,10},{13,12},{... | collective-permute-start | bytes 8072 | tf_op jit(solution)/shard_map/ppermute | solution.py:29
  191.9 5.5 %collective-permute-start.18 = (f32[1,3,224]{2,1,0:T(4,128)S(1)}, f32[1,3,224]{2,1,0:T(4,128)S(1)}, u32[]{:S(2)}, u32[]{:S(2)}) collective-permute-start(f32[1,3,224]{2,1,0:T(4,128)S(1)} %maximum_bitcast_fusion.18), channel_id=1, source_target_pairs={{0,1},{1,2},{2,3},{4,5},{5,6},{6,7},{8,9},{9,10},{10,11},{12,13},{... | collective-permute-start | bytes 8072 | tf_op jit(solution)/shard_map/ppermute | solution.py:28

commit v2 on v1

--- a/solution.py
+++ b/solution.py
@@ -124,19 +124,26 @@
 def spread_ghosts(rows, ghost_index):
     sizes = ghost_sizes()
     starts = ghost_offsets()
-    sends = [
-        jnp.take(rows, ghost_index[starts[d] : starts[d] + sizes[d]], axis=1) for d in range(8)
-    ]
+    order = [(-1, 0), (-1, -1), (-1, 1), (1, 0), (1, -1), (1, 1), (0, -1), (0, 1)]
+    picks = []
+    for p, q in order:
+        d = DIRECTIONS.index((p, q))
+        picks.append(ghost_index[starts[d] : starts[d] + sizes[d]])
+    sent = jnp.take(rows, jnp.concatenate(picks), axis=1)
+    bounds = [0]
+    for p, q in order:
+        bounds.append(bounds[-1] + sizes[DIRECTIONS.index((p, q))])
 
     def toward(p, q):
-        return sends[DIRECTIONS.index((p, q))]
+        k = order.index((p, q))
+        return sent[:, bounds[k] : bounds[k + 1]]
 
     got = {}
     face_x = GHOST_X
     corner = GHOST_C
     face_y = GHOST_Y
-    toward_low = jnp.concatenate([toward(-1, 0), toward(-1, -1), toward(-1, 1)], axis=1)
-    toward_high = jnp.concatenate([toward(1, 0), toward(1, -1), toward(1, 1)], axis=1)
+    toward_low = sent[:, bounds[0] : bounds[3]]
+    toward_high = sent[:, bounds[3] : bounds[6]]
     along_x = extended(jnp.stack([toward_low, toward_high]), (("gx", 0),), 1)
     from_low = along_x[0]
     from_high = along_x[3]

time: 211 us -> 197 us (0.934)
  the two profiles are of different devices: /device:TPU:20 before, /device:TPU:27 now
where the time goes in v2:
time: 197 us; the launch traced here: 199 us
  starting transfers between devices  53.3 us (27%)
  matrix products  39.3 us (20%)
  local copies, waits for them, and re-layouts  37.9 us (19%)
  waiting for transfers between devices  37.9 us (19%)
  other arithmetic  24.2 us (12%)
  between operations  5.4 us (3%)
    dot_general x10, matrix products, fold_batch(): jnp.einsum('rtb,tab->rta', qsel, weight, precision=lax.Precision.HIGH, pr...  36.7 us
    ppermute x10, starting transfers between devices, extended(): before = lax.ppermute(last, axis, up)  24.8 us
    ppermute x10, starting transfers between devices, extended(): after = lax.ppermute(leading, axis, down)  22.3 us
    ppermute x10, waiting for transfers between devices, extended(): after = lax.ppermute(leading, axis, down)  19 us
    ppermute x10, waiting for transfers between devices, extended(): before = lax.ppermute(last, axis, up)  16.9 us
    gather x5, local copies, waits for them, and re-layouts, spread_ghosts(): sent = jnp.take(rows, jnp.concatenate(picks), axis=1)  12 us
    dynamic_update_slice x2, other arithmetic, hydro_step(): stored = lax.dynamic_update_slice_in_dim(stored, weight, offset, 0)  6.18 us
    all_to_all x1, starting transfers between devices, mesh_max(): return jnp.max(lax.all_to_all(spread, ('gx', 'gy'), 0, 0, tiled=True))  6.11 us
  transfers between devices with their start and end apart: 21, of which 13 were waited for; matrix products, arithmetic and copies ran while one was open for 4% of the time, Pallas kernels for 0%

profile of v2, /device:TPU:27, one launch (start us, length us, event | category | flops | bytes accessed | tf_op | source)
XLA Modules:
  0.0 198.5 jit_solution(13409656130967455650)
XLA Ops:
  10.2 3.7 %collective-permute-start = (f32[1,15,384]{1,2,0:T(8,128)S(1)}, f32[1,15,384]{1,2,0:T(8,128)S(1)}, u32[]{:S(2)}, u32[]{:S(2)}) collective-permute-start(f32[1,15,384]{1,2,0:T(8,128)S(1)} %get-tuple-element.626), channel_id=1, source_target_pairs={{0,4},{4,8},{8,12},{12,16},{16,20},{20,24},{24,28},{1,5},{5,9},{9,... | collective-permute-start | bytes 69128 | tf_op jit(solution)/shard_map/ppermute | solution.py:28
  17.1 6.1 %all-to-all-start = ((f32[32,1,1]{2,1,0:T(1,128)}), f32[32,1,1]{2,1,0:T(1,128)S(1)}, u32[]{:S(2)}, u32[]{:S(2)}) async-start(f32[32,1,1]{2,1,0:T(1,128)} %broadcast_in_dim.120), calls=%async_computation | async-start | bytes 32768 | tf_op jit(solution)/shard_map/all_to_all | solution.py:37
  29.6 3.1 %collective-permute-start.3 = (f32[1,15,224]{2,1,0:T(8,128)S(1)}, f32[1,15,224]{2,1,0:T(8,128)S(1)}, u32[]{:S(2)}, u32[]{:S(2)}) collective-permute-start(f32[1,15,224]{2,1,0:T(8,128)S(1)} %maximum_bitcast_fusion.1), channel_id=1, source_target_pairs={{1,0},{2,1},{3,2},{5,4},{6,5},{7,6},{9,8},{10,9},{11,10},{13,12},{... | collective-permute-start | bytes 40328 | tf_op jit(solution)/shard_map/ppermute | solution.py:29
  34.6 2.9 %collective-permute-done.2 = f32[1,15,224]{2,1,0:T(8,128)S(1)} collective-permute-done((f32[1,15,224]{2,1,0:T(8,128)S(1)}, f32[1,15,224]{2,1,0:T(8,128)S(1)}, u32[]{:S(2)}, u32[]{:S(2)}) %collective-permute-start.2) | collective-permute-done | bytes 13472 | tf_op jit(solution)/shard_map/ppermute | solution.py:28
  43.2 23.1 %while.57 = (s32[]{:T(128)}, f32[53,16,128]{2,1,0:T(8,128)S(1)}, f32[64,128,128]{2,1,0:T(8,128)}, s32[]{:T(128)}, s32[64]{0:T(128)S(1)}, /*index=5*/f32[3,25,128...) while((s32[]{:T(128)}, f32[53,16,128]{2,1,0:T(8,128)S(1)}, ...), condition=%wide.region_5.7_spmd.clone, body=%wide.region_4.6_spmd.clone.sunk | while | flops 221341216 | bytes 8103835 | solution.py:252
  44.9 3.1 %fusion.231 = f32[64,128,128]{2,1,0:T(8,128)} fusion(f32[64,128,128]{2,1,0:T(8,128)} %get-tuple-element.1072, s32[]{:T(128)S(6)} %select_n.197, f32[32,128]{1,0:T(8,128)S(1)} %bitcast.480, f32[32,128]{1,0:T(8,128)S(1)} %bitcast.486, f32[32,128]{1,0:T(8,128)S(1)} %bitcast.482, f32[32,128]{1,0:T(8,128)S(1)} %bitcast.488, f32[32,128]{1,0:T(8,128)S(1)} %bitcast.478, ...), kind=kLoop, calls=%fused_computation.18.clone.1 | loop fusion | flops 6291456 | bytes 2195460 | tf_op jit(solution)/shard_map/while/body/dynamic_update_slice | solution.py:247
  48.6 4.9 %fusion.229 = f32[53,32,128]{2,0,1:T(8,128)S(1)} fusion(f32[32,128]{1,0:T(8,128)S(1)} %bitcast.481, f32[32,128]{1,0:T(8,128)S(1)} %bitcast.487, f32[32,128]{1,0:T(8,128)S(1)} %bitcast.483, f32[32,128]{1,0:T(8,128)S(1)} %bitcast.489, f32[32,128]{1,0:T(8,128)S(1)} %bitcast.479, f32[32,128]{1,0:T(8,128)S(1)} %bitcast.485, ...), kind=kOutput, calls=%fused_computation.20.clone.1 | convolution fusion | flops 173232128 | bytes 1835040 | tf_op jit(solution)/shard_map/while/body/rtb,tab->rta/dot_general | solution.py:225
  56.4 3.1 %fusion.231 = f32[64,128,128]{2,1,0:T(8,128)} fusion(f32[64,128,128]{2,1,0:T(8,128)} %get-tuple-element.1072, s32[]{:T(128)S(6)} %select_n.197, f32[32,128]{1,0:T(8,128)S(1)} %bitcast.480, f32[32,128]{1,0:T(8,128)S(1)} %bitcast.486, f32[32,128]{1,0:T(8,128)S(1)} %bitcast.482, f32[32,128]{1,0:T(8,128)S(1)} %bitcast.488, f32[32,128]{1,0:T(8,128)S(1)} %bitcast.478, ...), kind=kLoop, calls=%fused_computation.18.clone.1 | loop fusion | flops 6291456 | bytes 2195460 | tf_op jit(solution)/shard_map/while/body/dynamic_update_slice | solution.py:247
  60.1 4.9 %fusion.229 = f32[53,32,128]{2,0,1:T(8,128)S(1)} fusion(f32[32,128]{1,0:T(8,128)S(1)} %bitcast.481, f32[32,128]{1,0:T(8,128)S(1)} %bitcast.487, f32[32,128]{1,0:T(8,128)S(1)} %bitcast.483, f32[32,128]{1,0:T(8,128)S(1)} %bitcast.489, f32[32,128]{1,0:T(8,128)S(1)} %bitcast.479, f32[32,128]{1,0:T(8,128)S(1)} %bitcast.485, ...), kind=kOutput, calls=%fused_computation.20.clone.1 | convolution fusion | flops 173232128 | bytes 1835040 | tf_op jit(solution)/shard_map/while/body/rtb,tab->rta/dot_general | solution.py:225
  70.4 5.2 %collective-permute-start.4 = (f32[1,3,384]{1,2,0:T(8,128)S(1)}, f32[1,3,384]{1,2,0:T(8,128)S(1)}, u32[]{:S(2)}, u32[]{:S(2)}) collective-permute-start(f32[1,3,384]{1,2,0:T(8,128)S(1)} %get-tuple-element.622), channel_id=1, source_target_pairs={{0,4},{4,8},{8,12},{12,16},{16,20},{20,24},{24,28},{1,5},{5,9},{9,... | collective-permute-start | bytes 13832 | tf_op jit(solution)/shard_map/ppermute | solution.py:28
  79.1 5.1 %collective-permute-done.5 = f32[1,3,384]{1,2,0:T(8,128)S(1)} collective-permute-done((f32[1,3,384]{1,2,0:T(8,128)S(1)}, f32[1,3,384]{1,2,0:T(8,128)S(1)}, u32[]{:S(2)}, u32[]{:S(2)}) %collective-permute-start.5) | collective-permute-done | bytes 4640 | tf_op jit(solution)/shard_map/ppermute | solution.py:29
  84.4 3.0 %collective-permute-start.7 = (f32[1,3,224]{2,1,0:T(4,128)S(1)}, f32[1,3,224]{2,1,0:T(4,128)S(1)}, u32[]{:S(2)}, u32[]{:S(2)}) collective-permute-start(f32[1,3,224]{2,1,0:T(4,128)S(1)} %maximum_bitcast_fusion.3), channel_id=1, source_target_pairs={{1,0},{2,1},{3,2},{5,4},{6,5},{7,6},{9,8},{10,9},{11,10},{13,12},{... | collective-permute-start | bytes 8072 | tf_op jit(solution)/shard_map/ppermute | solution.py:29
  89.3 2.8 %collective-permute-done.6 = f32[1,3,224]{2,1,0:T(4,128)S(1)} collective-permute-done((f32[1,3,224]{2,1,0:T(4,128)S(1)}, f32[1,3,224]{2,1,0:T(4,128)S(1)}, u32[]{:S(2)}, u32[]{:S(2)}) %collective-permute-start.6) | collective-permute-done | bytes 2720 | tf_op jit(solution)/shard_map/ppermute | solution.py:28
  92.7 10.0 %while.58 = (s32[]{:T(128)}, f32[7,16,128]{2,1,0:T(8,128)S(1)}, s32[]{:T(128)}, f32[64,128,128]{2,1,0:T(8,128)}, s32[64]{0:T(128)S(1)}, /*index=5*/f32[7,25,128]...) while((s32[]{:T(128)}, f32[7,16,128]{2,1,0:T(8,128)S(1)}, ...), condition=%wide.region_9.13_spmd.clone, body=%wide.region_8.12_spmd.clone.sunk | while | flops 27570436 | bytes 2790583 | solution.py:275
  94.0 3.4 %fusion.236 = f32[7,32,128]{2,0,1:T(8,128)S(1)} fusion(f32[64,128,128]{2,1,0:T(8,128)} %get-tuple-element.1123, s32[]{:T(128)S(6)} %select_n.199, f32[32,7,128]{2,1,0:T(8,128)S(1)} %gather_fusion.3, pred[32]{0:T(512)(128)(4,1)S(1)} %get-tuple-element.1022), kind=kOutput, calls=%fused_computation.57.clone.1 | convolution fusion | flops 22048768 | bytes 2326564 | tf_op jit(solution)/shard_map/while/body/rtb,tab->rta/dot_general | solution.py:225
  99.0 3.4 %fusion.236 = f32[7,32,128]{2,0,1:T(8,128)S(1)} fusion(f32[64,128,128]{2,1,0:T(8,128)} %get-tuple-element.1123, s32[]{:T(128)S(6)} %select_n.199, f32[32,7,128]{2,1,0:T(8,128)S(1)} %gather_fusion.3, pred[32]{0:T(512)(128)(4,1)S(1)} %get-tuple-element.1022), kind=kOutput, calls=%fused_computation.57.clone.1 | convolution fusion | flops 22048768 | bytes 2326564 | tf_op jit(solution)/shard_map/while/body/rtb,tab->rta/dot_general | solution.py:225
  105.8 3.2 %collective-permute-start.8 = (f32[1,3,384]{1,2,0:T(8,128)S(1)}, f32[1,3,384]{1,2,0:T(8,128)S(1)}, u32[]{:S(2)}, u32[]{:S(2)}) collective-permute-start(f32[1,3,384]{1,2,0:T(8,128)S(1)} %get-tuple-element.618), channel_id=1, source_target_pairs={{0,4},{4,8},{8,12},{12,16},{16,20},{20,24},{24,28},{1,5},{5,9},{9,... | collective-permute-start | bytes 13832 | tf_op jit(solution)/shard_map/ppermute | solution.py:28
  111.9 5.0 %collective-permute-done.9 = f32[1,3,384]{1,2,0:T(8,128)S(1)} collective-permute-done((f32[1,3,384]{1,2,0:T(8,128)S(1)}, f32[1,3,384]{1,2,0:T(8,128)S(1)}, u32[]{:S(2)}, u32[]{:S(2)}) %collective-permute-start.9) | collective-permute-done | bytes 4640 | tf_op jit(solution)/shard_map/ppermute | solution.py:29
  117.0 3.2 %collective-permute-start.11 = (f32[1,3,224]{2,1,0:T(4,128)S(1)}, f32[1,3,224]{2,1,0:T(4,128)S(1)}, u32[]{:S(2)}, u32[]{:S(2)}) collective-permute-start(f32[1,3,224]{2,1,0:T(4,128)S(1)} %maximum_bitcast_fusion.5), channel_id=1, source_target_pairs={{1,0},{2,1},{3,2},{5,4},{6,5},{7,6},{9,8},{10,9},{11,10},{13,12},{... | collective-permute-start | bytes 8072 | tf_op jit(solution)/shard_map/ppermute | solution.py:29
  125.4 10.0 %while.59 = (s32[]{:T(128)}, f32[7,16,128]{2,1,0:T(8,128)S(1)}, s32[]{:T(128)}, f32[64,128,128]{2,1,0:T(8,128)}, s32[64]{0:T(128)S(1)}, /*index=5*/f32[7,25,128]...) while((s32[]{:T(128)}, f32[7,16,128]{2,1,0:T(8,128)S(1)}, ...), condition=%wide.region_13.17_spmd.clone, body=%wide.region_12.16_spmd.clone.sunk | while | flops 27570436 | bytes 2790583 | solution.py:275
  126.7 3.4 %fusion.242 = f32[7,32,128]{2,0,1:T(8,128)S(1)} fusion(f32[64,128,128]{2,1,0:T(8,128)} %get-tuple-element.1159, s32[]{:T(128)S(6)} %select_n.201, f32[32,7,128]{2,1,0:T(8,128)S(1)} %gather_fusion.4, pred[32]{0:T(512)(128)(4,1)S(1)} %get-tuple-element.1033), kind=kOutput, calls=%fused_computation.78.clone.1 | convolution fusion | flops 22048768 | bytes 2326564 | tf_op jit(solution)/shard_map/while/body/rtb,tab->rta/dot_general | solution.py:225
  131.7 3.4 %fusion.242 = f32[7,32,128]{2,0,1:T(8,128)S(1)} fusion(f32[64,128,128]{2,1,0:T(8,128)} %get-tuple-element.1159, s32[]{:T(128)S(6)} %select_n.201, f32[32,7,128]{2,1,0:T(8,128)S(1)} %gather_fusion.4, pred[32]{0:T(512)(128)(4,1)S(1)} %get-tuple-element.1033), kind=kOutput, calls=%fused_computation.78.clone.1 | convolution fusion | flops 22048768 | bytes 2326564 | tf_op jit(solution)/shard_map/while/body/rtb,tab->rta/dot_general | solution.py:225
  138.5 3.2 %collective-permute-start.12 = (f32[1,3,384]{1,2,0:T(8,128)S(1)}, f32[1,3,384]{1,2,0:T(8,128)S(1)}, u32[]{:S(2)}, u32[]{:S(2)}) collective-permute-start(f32[1,3,384]{1,2,0:T(8,128)S(1)} %get-tuple-element.614), channel_id=1, source_target_pairs={{0,4},{4,8},{8,12},{12,16},{16,20},{20,24},{24,28},{1,5},{5,9},{9,... | collective-permute-start | bytes 13832 | tf_op jit(solution)/shard_map/ppermute | solution.py:28
  145.1 4.5 %collective-permute-done.13 = f32[1,3,384]{1,2,0:T(8,128)S(1)} collective-permute-done((f32[1,3,384]{1,2,0:T(8,128)S(1)}, f32[1,3,384]{1,2,0:T(8,128)S(1)}, u32[]{:S(2)}, u32[]{:S(2)}) %collective-permute-start.13) | collective-permute-done | bytes 4640 | tf_op jit(solution)/shard_map/ppermute | solution.py:29
  156.6 10.0 %while.60 = (s32[]{:T(128)}, f32[7,16,128]{2,1,0:T(8,128)S(1)}, s32[]{:T(128)}, f32[64,128,128]{2,1,0:T(8,128)}, s32[64]{0:T(128)S(1)}, /*index=5*/f32[7,25,128]...) while((s32[]{:T(128)}, f32[7,16,128]{2,1,0:T(8,128)S(1)}, ...), condition=%wide.region_17.21_spmd.clone, body=%wide.region_16.20_spmd.clone.sunk | while | flops 27570436 | bytes 2790583 | solution.py:275
  158.0 3.4 %fusion.248 = f32[7,32,128]{2,0,1:T(8,128)S(1)} fusion(f32[64,128,128]{2,1,0:T(8,128)} %get-tuple-element.1195, s32[]{:T(128)S(6)} %select_n.203, f32[32,7,128]{2,1,0:T(8,128)S(1)} %gather_fusion.5, pred[32]{0:T(512)(128)(4,1)S(1)} %get-tuple-element.1044), kind=kOutput, calls=%fused_computation.99.clone.1 | convolution fusion | flops 22048768 | bytes 2326564 | tf_op jit(solution)/shard_map/while/body/rtb,tab->rta/dot_general | solution.py:225
  163.0 3.4 %fusion.248 = f32[7,32,128]{2,0,1:T(8,128)S(1)} fusion(f32[64,128,128]{2,1,0:T(8,128)} %get-tuple-element.1195, s32[]{:T(128)S(6)} %select_n.203, f32[32,7,128]{2,1,0:T(8,128)S(1)} %gather_fusion.5, pred[32]{0:T(512)(128)(4,1)S(1)} %get-tuple-element.1044), kind=kOutput, calls=%fused_computation.99.clone.1 | convolution fusion | flops 22048768 | bytes 2326564 | tf_op jit(solution)/shard_map/while/body/rtb,tab->rta/dot_general | solution.py:225
  169.8 3.2 %collective-permute-start.16 = (f32[1,3,384]{1,2,0:T(8,128)S(1)}, f32[1,3,384]{1,2,0:T(8,128)S(1)}, u32[]{:S(2)}, u32[]{:S(2)}) collective-permute-start(f32[1,3,384]{1,2,0:T(8,128)S(1)} %get-tuple-element.610), channel_id=1, source_target_pairs={{0,4},{4,8},{8,12},{12,16},{16,20},{20,24},{24,28},{1,5},{5,9},{9,... | collective-permute-start | bytes 13832 | tf_op jit(solution)/shard_map/ppermute | solution.py:28
  176.4 4.5 %collective-permute-done.17 = f32[1,3,384]{1,2,0:T(8,128)S(1)} collective-permute-done((f32[1,3,384]{1,2,0:T(8,128)S(1)}, f32[1,3,384]{1,2,0:T(8,128)S(1)}, u32[]{:S(2)}, u32[]{:S(2)}) %collective-permute-start.17) | collective-permute-done | bytes 4640 | tf_op jit(solution)/shard_map/ppermute | solution.py:29
  187.8 10.0 %while.61 = (s32[]{:T(128)}, f32[7,16,128]{2,1,0:T(8,128)S(1)}, s32[]{:T(128)}, f32[64,128,128]{2,1,0:T(8,128)}, s32[64]{0:T(128)S(1)}, /*index=5*/f32[7,25,128]...) while((s32[]{:T(128)}, f32[7,16,128]{2,1,0:T(8,128)S(1)}, ...), condition=%wide.region_21.25_spmd.clone, body=%wide.region_20.24_spmd.clone.sunk | while | flops 27570436 | bytes 2790583 | solution.py:275
  189.2 3.4 %fusion.254 = f32[7,32,128]{2,0,1:T(8,128)S(1)} fusion(f32[64,128,128]{2,1,0:T(8,128)} %get-tuple-element.1231, s32[]{:T(128)S(6)} %select_n.205, f32[32,7,128]{2,1,0:T(8,128)S(1)} %gather_fusion.6, pred[32]{0:T(512)(128)(4,1)S(1)} %get-tuple-element.1055), kind=kOutput, calls=%fused_computation.120.clone.1 | convolution fusion | flops 22048768 | bytes 2326564 | tf_op jit(solution)/shard_map/while/body/rtb,tab->rta/dot_general | solution.py:225
  194.2 3.4 %fusion.254 = f32[7,32,128]{2,0,1:T(8,128)S(1)} fusion(f32[64,128,128]{2,1,0:T(8,128)} %get-tuple-element.1231, s32[]{:T(128)S(6)} %select_n.205, f32[32,7,128]{2,1,0:T(8,128)S(1)} %gather_fusion.6, pred[32]{0:T(512)(128)(4,1)S(1)} %get-tuple-element.1055), kind=kOutput, calls=%fused_computation.120.clone.1 | convolution fusion | flops 22048768 | bytes 2326564 | tf_op jit(solution)/shard_map/while/body/rtb,tab->rta/dot_general | solution.py:225
  (354 shorter events, 91.3 us)
Async XLA Ops:
  10.2 19.1 %collective-permute-start = (f32[1,15,384]{1,2,0:T(8,128)S(1)}, f32[1,15,384]{1,2,0:T(8,128)S(1)}, u32[]{:S(2)}, u32[]{:S(2)}) collective-permute-start(f32[1,15,384]{1,2,0:T(8,128)S(1)} %get-tuple-element.626), channel_id=1, source_target_pairs={{0,4},{4,8},{8,12},{12,16},{16,20},{20,24},{24,28},{1,5},{5,9},{9,... | collective-permute-start | bytes 69128 | tf_op jit(solution)/shard_map/ppermute | solution.py:28
  13.9 15.5 %collective-permute-start.1 = (f32[1,15,384]{1,2,0:T(8,128)S(1)}, f32[1,15,384]{1,2,0:T(8,128)S(1)}, u32[]{:S(2)}, u32[]{:S(2)}) collective-permute-start(f32[1,15,384]{1,2,0:T(8,128)S(1)} %get-tuple-element.627), channel_id=1, source_target_pairs={{4,0},{8,4},{12,8},{16,12},{20,16},{24,20},{28,24},{5,1},{9,5},{13... | collective-permute-start | bytes 69128 | tf_op jit(solution)/shard_map/ppermute | solution.py:29
  17.1 8.9 %all-to-all-start = ((f32[32,1,1]{2,1,0:T(1,128)}), f32[32,1,1]{2,1,0:T(1,128)S(1)}, u32[]{:S(2)}, u32[]{:S(2)}) async-start(f32[32,1,1]{2,1,0:T(1,128)} %broadcast_in_dim.120), calls=%async_computation | async-start | bytes 32768 | tf_op jit(solution)/shard_map/all_to_all | solution.py:37
  29.6 4.9 %collective-permute-start.3 = (f32[1,15,224]{2,1,0:T(8,128)S(1)}, f32[1,15,224]{2,1,0:T(8,128)S(1)}, u32[]{:S(2)}, u32[]{:S(2)}) collective-permute-start(f32[1,15,224]{2,1,0:T(8,128)S(1)} %maximum_bitcast_fusion.1), channel_id=1, source_target_pairs={{1,0},{2,1},{3,2},{5,4},{6,5},{7,6},{9,8},{10,9},{11,10},{13,12},{... | collective-permute-start | bytes 40328 | tf_op jit(solution)/shard_map/ppermute | solution.py:29
  32.9 4.5 %collective-permute-start.2 = (f32[1,15,224]{2,1,0:T(8,128)S(1)}, f32[1,15,224]{2,1,0:T(8,128)S(1)}, u32[]{:S(2)}, u32[]{:S(2)}) collective-permute-start(f32[1,15,224]{2,1,0:T(8,128)S(1)} %maximum_bitcast_fusion), channel_id=1, source_target_pairs={{0,1},{1,2},{2,3},{4,5},{5,6},{6,7},{8,9},{9,10},{10,11},{12,13},{... | collective-permute-start | bytes 40328 | tf_op jit(solution)/shard_map/ppermute | solution.py:28
  40.6 2.5 %copy-start = (s32[64]{0:T(128)S(1)}, s32[64]{0:T(128)}, u32[]{:S(2)}) copy-start(s32[64]{0:T(128)} %param.36) | copy-start | bytes 772
  40.7 2.5 %copy-start.7 = (s32[64]{0:T(128)S(1)}, s32[64]{0:T(128)}, u32[]{:S(2)}) copy-start(s32[64]{0:T(128)} %param.35) | copy-start | bytes 772
  43.2 23.2 %copy-start.5 = (f32[3,2048]{1,0:T(4,128)S(1)}, f32[3,2048]{1,0:T(4,128)}, u32[]{:S(2)}) copy-start(f32[3,2048]{1,0:T(4,128)} %param.27) | copy-start | bytes 73732
  43.2 23.5 %copy-start.1 = (f32[3,2048]{1,0:T(4,128)S(1)}, f32[3,2048]{1,0:T(4,128)}, u32[]{:S(2)}) copy-start(f32[3,2048]{1,0:T(4,128)} %param.30) | copy-start | bytes 73732
  43.2 23.5 %copy-start.3 = (f32[3,2048]{1,0:T(4,128)S(1)}, f32[3,2048]{1,0:T(4,128)}, u32[]{:S(2)}) copy-start(f32[3,2048]{1,0:T(4,128)} %param.29) | copy-start | bytes 73732
  66.5 9.1 %copy-start.2 = (f32[2048]{0:T(1024)S(1)}, f32[2048]{0:T(1024)}, u32[]{:S(2)}) copy-start(f32[2048]{0:T(1024)} %param.32) | copy-start | bytes 24580
  66.6 9.1 %copy-start.6 = (f32[2048]{0:T(1024)S(1)}, f32[2048]{0:T(1024)}, u32[]{:S(2)}) copy-start(f32[2048]{0:T(1024)} %param.31) | copy-start | bytes 24580
  66.7 11.7 %copy-start.4 = (f32[2048]{0:T(1024)S(1)}, f32[2048]{0:T(1024)}, u32[]{:S(2)}) copy-start(f32[2048]{0:T(1024)} %param.28) | copy-start | bytes 24580
  70.4 8.6 %collective-permute-start.4 = (f32[1,3,384]{1,2,0:T(8,128)S(1)}, f32[1,3,384]{1,2,0:T(8,128)S(1)}, u32[]{:S(2)}, u32[]{:S(2)}) collective-permute-start(f32[1,3,384]{1,2,0:T(8,128)S(1)} %get-tuple-element.622), channel_id=1, source_target_pairs={{0,4},{4,8},{8,12},{12,16},{16,20},{20,24},{24,28},{1,5},{5,9},{9,... | collective-permute-start | bytes 13832 | tf_op jit(solution)/shard_map/ppermute | solution.py:28
  76.4 7.9 %collective-permute-start.5 = (f32[1,3,384]{1,2,0:T(8,128)S(1)}, f32[1,3,384]{1,2,0:T(8,128)S(1)}, u32[]{:S(2)}, u32[]{:S(2)}) collective-permute-start(f32[1,3,384]{1,2,0:T(8,128)S(1)} %get-tuple-element.623), channel_id=1, source_target_pairs={{4,0},{8,4},{12,8},{16,12},{20,16},{24,20},{28,24},{5,1},{9,5},{13... | collective-permute-start | bytes 13832 | tf_op jit(solution)/shard_map/ppermute | solution.py:29
  84.4 4.8 %collective-permute-start.7 = (f32[1,3,224]{2,1,0:T(4,128)S(1)}, f32[1,3,224]{2,1,0:T(4,128)S(1)}, u32[]{:S(2)}, u32[]{:S(2)}) collective-permute-start(f32[1,3,224]{2,1,0:T(4,128)S(1)} %maximum_bitcast_fusion.3), channel_id=1, source_target_pairs={{1,0},{2,1},{3,2},{5,4},{6,5},{7,6},{9,8},{10,9},{11,10},{13,12},{... | collective-permute-start | bytes 8072 | tf_op jit(solution)/shard_map/ppermute | solution.py:29
  87.7 4.4 %collective-permute-start.6 = (f32[1,3,224]{2,1,0:T(4,128)S(1)}, f32[1,3,224]{2,1,0:T(4,128)S(1)}, u32[]{:S(2)}, u32[]{:S(2)}) collective-permute-start(f32[1,3,224]{2,1,0:T(4,128)S(1)} %maximum_bitcast_fusion.2), channel_id=1, source_target_pairs={{0,1},{1,2},{2,3},{4,5},{5,6},{6,7},{8,9},{9,10},{10,11},{12,13},{... | collective-permute-start | bytes 8072 | tf_op jit(solution)/shard_map/ppermute | solution.py:28
  105.8 6.0 %collective-permute-start.8 = (f32[1,3,384]{1,2,0:T(8,128)S(1)}, f32[1,3,384]{1,2,0:T(8,128)S(1)}, u32[]{:S(2)}, u32[]{:S(2)}) collective-permute-start(f32[1,3,384]{1,2,0:T(8,128)S(1)} %get-tuple-element.618), channel_id=1, source_target_pairs={{0,4},{4,8},{8,12},{12,16},{16,20},{20,24},{24,28},{1,5},{5,9},{9,... | collective-permute-start | bytes 13832 | tf_op jit(solution)/shard_map/ppermute | solution.py:28
  109.0 7.9 %collective-permute-start.9 = (f32[1,3,384]{1,2,0:T(8,128)S(1)}, f32[1,3,384]{1,2,0:T(8,128)S(1)}, u32[]{:S(2)}, u32[]{:S(2)}) collective-permute-start(f32[1,3,384]{1,2,0:T(8,128)S(1)} %get-tuple-element.619), channel_id=1, source_target_pairs={{4,0},{8,4},{12,8},{16,12},{20,16},{24,20},{28,24},{5,1},{9,5},{13... | collective-permute-start | bytes 13832 | tf_op jit(solution)/shard_map/ppermute | solution.py:29
  117.0 5.0 %collective-permute-start.11 = (f32[1,3,224]{2,1,0:T(4,128)S(1)}, f32[1,3,224]{2,1,0:T(4,128)S(1)}, u32[]{:S(2)}, u32[]{:S(2)}) collective-permute-start(f32[1,3,224]{2,1,0:T(4,128)S(1)} %maximum_bitcast_fusion.5), channel_id=1, source_target_pairs={{1,0},{2,1},{3,2},{5,4},{6,5},{7,6},{9,8},{10,9},{11,10},{13,12},{... | collective-permute-start | bytes 8072 | tf_op jit(solution)/shard_map/ppermute | solution.py:29
  120.5 4.4 %collective-permute-start.10 = (f32[1,3,224]{2,1,0:T(4,128)S(1)}, f32[1,3,224]{2,1,0:T(4,128)S(1)}, u32[]{:S(2)}, u32[]{:S(2)}) collective-permute-start(f32[1,3,224]{2,1,0:T(4,128)S(1)} %maximum_bitcast_fusion.4), channel_id=1, source_target_pairs={{0,1},{1,2},{2,3},{4,5},{5,6},{6,7},{8,9},{9,10},{10,11},{12,13},{... | collective-permute-start | bytes 8072 | tf_op jit(solution)/shard_map/ppermute | solution.py:28
  138.5 6.5 %collective-permute-start.12 = (f32[1,3,384]{1,2,0:T(8,128)S(1)}, f32[1,3,384]{1,2,0:T(8,128)S(1)}, u32[]{:S(2)}, u32[]{:S(2)}) collective-permute-start(f32[1,3,384]{1,2,0:T(8,128)S(1)} %get-tuple-element.614), channel_id=1, source_target_pairs={{0,4},{4,8},{8,12},{12,16},{16,20},{20,24},{24,28},{1,5},{5,9},{9,... | collective-permute-start | bytes 13832 | tf_op jit(solution)/shard_map/ppermute | solution.py:28
  141.7 7.9 %collective-permute-start.13 = (f32[1,3,384]{1,2,0:T(8,128)S(1)}, f32[1,3,384]{1,2,0:T(8,128)S(1)}, u32[]{:S(2)}, u32[]{:S(2)}) collective-permute-start(f32[1,3,384]{1,2,0:T(8,128)S(1)} %get-tuple-element.615), channel_id=1, source_target_pairs={{4,0},{8,4},{12,8},{16,12},{20,16},{24,20},{28,24},{5,1},{9,5},{13... | collective-permute-start | bytes 13832 | tf_op jit(solution)/shard_map/ppermute | solution.py:29
  149.8 3.4 %collective-permute-start.15 = (f32[1,3,224]{2,1,0:T(4,128)S(1)}, f32[1,3,224]{2,1,0:T(4,128)S(1)}, u32[]{:S(2)}, u32[]{:S(2)}) collective-permute-start(f32[1,3,224]{2,1,0:T(4,128)S(1)} %maximum_bitcast_fusion.7), channel_id=1, source_target_pairs={{1,0},{2,1},{3,2},{5,4},{6,5},{7,6},{9,8},{10,9},{11,10},{13,12},{... | collective-permute-start | bytes 8072 | tf_op jit(solution)/shard_map/ppermute | solution.py:29
  151.7 4.4 %collective-permute-start.14 = (f32[1,3,224]{2,1,0:T(4,128)S(1)}, f32[1,3,224]{2,1,0:T(4,128)S(1)}, u32[]{:S(2)}, u32[]{:S(2)}) collective-permute-start(f32[1,3,224]{2,1,0:T(4,128)S(1)} %maximum_bitcast_fusion.6), channel_id=1, source_target_pairs={{0,1},{1,2},{2,3},{4,5},{5,6},{6,7},{8,9},{9,10},{10,11},{12,13},{... | collective-permute-start | bytes 8072 | tf_op jit(solution)/shard_map/ppermute | solution.py:28
  169.8 6.5 %collective-permute-start.16 = (f32[1,3,384]{1,2,0:T(8,128)S(1)}, f32[1,3,384]{1,2,0:T(8,128)S(1)}, u32[]{:S(2)}, u32[]{:S(2)}) collective-permute-start(f32[1,3,384]{1,2,0:T(8,128)S(1)} %get-tuple-element.610), channel_id=1, source_target_pairs={{0,4},{4,8},{8,12},{12,16},{16,20},{20,24},{24,28},{1,5},{5,9},{9,... | collective-permute-start | bytes 13832 | tf_op jit(solution)/shard_map/ppermute | solution.py:28
  172.9 7.9 %collective-permute-start.17 = (f32[1,3,384]{1,2,0:T(8,128)S(1)}, f32[1,3,384]{1,2,0:T(8,128)S(1)}, u32[]{:S(2)}, u32[]{:S(2)}) collective-permute-start(f32[1,3,384]{1,2,0:T(8,128)S(1)} %get-tuple-element.611), channel_id=1, source_target_pairs={{4,0},{8,4},{12,8},{16,12},{20,16},{24,20},{28,24},{5,1},{9,5},{13... | collective-permute-start | bytes 13832 | tf_op jit(solution)/shard_map/ppermute | solution.py:29
  181.0 3.4 %collective-permute-start.19 = (f32[1,3,224]{2,1,0:T(4,128)S(1)}, f32[1,3,224]{2,1,0:T(4,128)S(1)}, u32[]{:S(2)}, u32[]{:S(2)}) collective-permute-start(f32[1,3,224]{2,1,0:T(4,128)S(1)} %maximum_bitcast_fusion.9), channel_id=1, source_target_pairs={{1,0},{2,1},{3,2},{5,4},{6,5},{7,6},{9,8},{10,9},{11,10},{13,12},{... | collective-permute-start | bytes 8072 | tf_op jit(solution)/shard_map/ppermute | solution.py:29
  182.9 4.4 %collective-permute-start.18 = (f32[1,3,224]{2,1,0:T(4,128)S(1)}, f32[1,3,224]{2,1,0:T(4,128)S(1)}, u32[]{:S(2)}, u32[]{:S(2)}) collective-permute-start(f32[1,3,224]{2,1,0:T(4,128)S(1)} %maximum_bitcast_fusion.8), channel_id=1, source_target_pairs={{0,1},{1,2},{2,3},{4,5},{5,6},{6,7},{8,9},{9,10},{10,11},{12,13},{... | collective-permute-start | bytes 8072 | tf_op jit(solution)/shard_map/ppermute | solution.py:28
